TPU v7x, 32 devices: a whole 2x2x4 slice. The times are simulated.
32 devices in a mesh: param: 4 (over y, core), ex: 8 (over z, x).
Axes of the slice: x: 2, y: 2, z: 4, core: 2. Of those that a mesh axis runs over, the one named last changes fastest.
Arguments:
- activations: bfloat16 [32, 128, 8192], P('ex', None, 'param'), may hold values from -6 to 6
- out_grads: bfloat16 [32, 128, 8192], P('ex', None, 'param'), may hold values from -6 to 6
- proj_in: bfloat16 [8192, 32], P('param'), may hold values from -0.0625 to 0.0625
- proj_out: bfloat16 [8192, 32], P('param'), may hold values from -0.0625 to 0.0625
- prior: float32 [1024, 1024], P('ex', 'param'), as said below
- probes: bfloat16 [512, 1024], P(('param', 'ex')), may hold values from -6 to 6
Outputs:
- scores: float32 [512, 32], P('param', 'ex')
Inputs may be any that keep to these rules, and one draw needn't show every extreme that they name: prior is symmetric positive definite with smallest eigenvalue at least 0.1.
All inputs are finite; a program needn't handle non-finite values.
Results may differ from a plain program's by a relative error of at most 0.0042.
Values may be sent and summed in bfloat16 or wider, within the bound.
No kernel may reach another device: no remote copies, remote signals or barrier semaphores. Data moves between devices by JAX's collectives and lax.ppermute only.
A program may use at most 64 MiB of HBM per device.

v0:
```python
import math

import jax
import jax.numpy as jnp
from jax import lax
from jax.experimental import pallas as pl
from jax.experimental.pallas import tpu as pltpu
from jax.sharding import PartitionSpec as P


def _inverse_factor_kernel(a_ref, w_ref, s_ref):
    n = a_ref.shape[0]
    s_ref[...] = a_ref[...]
    rows = lax.broadcasted_iota(jnp.int32, (n, n), 0)
    cols = lax.broadcasted_iota(jnp.int32, (n, n), 1)
    w_ref[...] = jnp.where(rows == cols, 1.0, 0.0).astype(jnp.float32)
    for group in range(n // 8):
        low = group * 8

        def step(t, carry):
            j = low + t
            pivot_row = s_ref[pl.ds(j, 1), :]
            inverse_row = w_ref[pl.ds(j, 1), :]
            lane = lax.broadcasted_iota(jnp.int32, (1, n), 1)
            pivot = jnp.sum(jnp.where(lane == j, pivot_row, 0.0), axis=1, keepdims=True)
            scale = 1.0 / jnp.sqrt(pivot)
            pivot_row = pivot_row * scale
            inverse_row = inverse_row * scale
            rest = s_ref[low:, :]
            lanes = lax.broadcasted_iota(jnp.int32, rest.shape, 1)
            column = jnp.sum(jnp.where(lanes == j, rest, 0.0), axis=1, keepdims=True)
            below = lax.broadcasted_iota(jnp.int32, (n - low, 1), 0) + low
            factor = jnp.where(below > j, column * scale, 0.0)
            s_ref[low:, :] = rest - factor * pivot_row
            w_ref[low:, :] = w_ref[low:, :] - factor * inverse_row
            s_ref[pl.ds(j, 1), :] = pivot_row
            w_ref[pl.ds(j, 1), :] = inverse_row
            return carry

        lax.fori_loop(0, 8, step, 0)


def inverse_factor(block):
    n = block.shape[0]
    return pl.pallas_call(
        _inverse_factor_kernel,
        out_shape=jax.ShapeDtypeStruct((n, n), jnp.float32),
        in_specs=[pl.BlockSpec(memory_space=pltpu.VMEM)],
        out_specs=pl.BlockSpec(memory_space=pltpu.VMEM),
        scratch_shapes=[pltpu.VMEM((n, n), jnp.float32)],
    )(block)


def outer_terms(factors, in_width):
    first = factors[:, :in_width]
    second = factors[:, in_width:]
    product = jnp.einsum("eol,eil->eoi", second, first, precision=lax.Precision.HIGHEST)
    return product.reshape(product.shape[0], -1)


def spd_solve(matrix, rhs_t):
    lower_factor = jnp.linalg.cholesky(matrix)
    halfway = lax.linalg.triangular_solve(lower_factor, rhs_t, left_side=True, lower=True)
    return lax.linalg.triangular_solve(
        lower_factor, halfway, left_side=True, lower=True, transpose_a=True
    )


def mm(a, b):
    return jnp.dot(a, b, precision=lax.Precision.HIGHEST, preferred_element_type=jnp.float32)


def blocked_cholesky(matrix, block):
    count = matrix.shape[0] // block
    inverses, panels = [], []
    trailing = matrix
    for k in range(count):
        inverse = inverse_factor(trailing[:block, :block])
        inverses.append(inverse)
        if k + 1 < count:
            panel = mm(trailing[block:, :block], inverse.T)
            panels.append(panel)
            trailing = trailing[block:, block:] - mm(panel, panel.T)
    return inverses, panels


def blocked_solve(inverses, panels, rhs, block):
    count = len(inverses)
    parts = []
    rest = rhs
    for k in range(count):
        part = mm(inverses[k], rest[:block])
        parts.append(part)
        if k + 1 < count:
            rest = rest[block:] - mm(panels[k], part)
    done = None
    for k in reversed(range(count)):
        target = parts[k]
        if done is not None:
            target = target - mm(panels[k].T, done)
        part = mm(inverses[k].T, target)
        done = part if done is None else jnp.concatenate((part, done), axis=0)
    return done


def gather_rows(block_rows, axis_name):
    count = lax.axis_size(axis_name)
    rows = block_rows.shape[0]
    padded = jnp.zeros((count * rows,) + block_rows.shape[1:], block_rows.dtype)
    padded = lax.dynamic_update_slice_in_dim(padded, block_rows, lax.axis_index(axis_name) * rows, 0)
    return lax.psum(padded, axis_name)


def gather_prior(prior):
    n_ex = lax.axis_size("ex")
    n_par = lax.axis_size("param")
    rows, cols = prior.shape
    blocks = lax.all_gather(prior, ("ex", "param"), axis=0, tiled=False)
    blocks = blocks.reshape(n_ex, n_par, rows, cols).transpose(0, 2, 1, 3)
    return blocks.reshape(n_ex * rows, n_par * cols)


def per_device(activations, out_grads, proj_in, proj_out, prior, probes):
    full_prior = gather_prior(prior)
    tokens = activations.shape[1]
    in_width = proj_in.shape[1]
    factor_in = jnp.einsum("eld,dk->ekl", activations, proj_in, preferred_element_type=jnp.float32)
    factor_out = jnp.einsum("eld,dk->ekl", out_grads, proj_out, preferred_element_type=jnp.float32)
    factors = jnp.concatenate((factor_in, factor_out), axis=1)
    factors = lax.psum(factors, "param")
    summed = outer_terms(factors, in_width)
    features = (summed * (1.0 / math.sqrt(tokens))).astype(jnp.bfloat16)
    local_count, feat_dim = features.shape
    all_features = gather_rows(features.astype(jnp.float32), "ex")
    train_count = all_features.shape[0]
    block = 128 if feat_dim % 128 == 0 else feat_dim
    inverses, panels = blocked_cholesky(full_prior, block)
    prior_solved_t = blocked_solve(inverses, panels, all_features.T, block)
    gram = jnp.dot(all_features, prior_solved_t, precision=lax.Precision.HIGHEST)
    small = gram + train_count * jnp.eye(train_count, dtype=jnp.float32)
    small_inverse = inverse_factor(small)
    solved_all = train_count * mm(small_inverse.T, mm(small_inverse, prior_solved_t.T))
    solved_all = solved_all.astype(jnp.bfloat16)
    row_start = lax.axis_index("ex") * local_count
    solved = lax.dynamic_slice_in_dim(solved_all, row_start, local_count, 0)
    inverse_root = 1.0 / math.sqrt(feat_dim)
    block_probes = gather_rows(probes.astype(jnp.float32), "ex")
    return mm(block_probes, solved.astype(jnp.float32).T) * inverse_root


def solution(mesh):
    return jax.shard_map(
        per_device,
        mesh=mesh,
        in_specs=(
            P("ex", None, "param"),
            P("ex", None, "param"),
            P("param", None),
            P("param", None),
            P("ex", "param"),
            P(("param", "ex"), None),
        ),
        out_specs=P("param", "ex"),
        check_vma=False,
    )
```

profile of v0, /device:TPU:0, one launch (start us, length us, event | category | flops | bytes accessed | tf_op | source)
XLA Modules:
  0.0 291.5 jit_solution(13142668678937136410)
XLA Ops:
  7.4 1.6 copy-done
  9.0 1.8 convolution_bitcast_fusion
  12.9 34.4 %all-reduce.4.cloned.1.call-done = f32[4,64,128]{2,1,0:T(8,128)} async-done(((f32[4,64,128]{2,1,0:T(8,128)}), f32[4,64,128]{2,1,0:T(8,128)}) %all-reduce.4.cloned.1.call-update) | async-done | bytes 131088 | tf_op jit(solution)/shard_map/psum | solution.py:130
  49.2 32.2 %all-gather.3.cloned.1.call-done = f32[4096,256]{1,0:T(8,128)} async-done(((f32[128,256]{1,0:T(8,128)}), f32[4096,256]{1,0:T(8,128)}) %all-gather.3.cloned.1.call-update) | async-done | bytes 4194320 | tf_op jit(solution)/shard_map/all_gather | solution.py:118
  81.4 4.9 %copy.7 = f32[8,4,128,256]{3,1,2,0:T(4,128)S(1)} copy(f32[8,4,128,256]{3,2,1,0:T(8,128)} %bitcast.106) | data formatting | bytes 8388608 | tf_op jit(solution)/shard_map/reshape | solution.py:119
  87.4 2.0 copy-done.1
  89.9 15.0 %shard_map.64 = f32[128,128]{1,0:T(8,128)} custom-call(f32[128,128]{1,0:T(8,128)} %slice.151.a_ref), custom_call_target="tpu_custom_call" | custom-call | tf_op jit(solution)/shard_map/pallas_call | solution.py:45
  106.5 4.8 %slice_subtract_fusion = f32[896,896]{1,0:T(8,128)S(1)} fusion(f32[1024,1024]{1,0:T(8,128)} %bitcast.105, f32[896,128]{1,0:T(8,128)S(1)} %fusion.3), kind=kOutput, calls=%fused_computation | convolution fusion | flops 1233928192 | bytes 7340032 | tf_op jit(solution)/shard_map/dot_general | solution.py:70
  111.4 1.6 copy-done.2
  113.6 15.0 %shard_map.65 = f32[128,128]{1,0:T(8,128)} custom-call(f32[128,128]{1,0:T(8,128)} %slice.154.a_ref), custom_call_target="tpu_custom_call" | custom-call | tf_op jit(solution)/shard_map/pallas_call | solution.py:45
  130.1 3.7 %slice_subtract_fusion.1 = f32[768,768]{1,0:T(8,128)S(1)} fusion(f32[896,896]{1,0:T(8,128)} %copy-done.2, f32[768,128]{1,0:T(8,128)S(1)} %fusion.5), kind=kOutput, calls=%fused_computation.1 | convolution fusion | flops 906559488 | bytes 5505024 | tf_op jit(solution)/shard_map/dot_general | solution.py:70
  135.9 15.0 %shard_map.66 = f32[128,128]{1,0:T(8,128)} custom-call(f32[128,128]{1,0:T(8,128)} %slice.159.a_ref), custom_call_target="tpu_custom_call" | custom-call | tf_op jit(solution)/shard_map/pallas_call | solution.py:45
  152.3 2.9 slice_subtract_fusion.2
  157.0 15.2 %shard_map.67 = f32[128,128]{1,0:T(8,128)} custom-call(f32[128,128]{1,0:T(8,128)} %slice.164.a_ref), custom_call_target="tpu_custom_call" | custom-call | tf_op jit(solution)/shard_map/pallas_call | solution.py:45
  183.1 15.0 %shard_map.68 = f32[128,128]{1,0:T(8,128)} custom-call(f32[128,128]{1,0:T(8,128)} %slice.169.a_ref), custom_call_target="tpu_custom_call" | custom-call | tf_op jit(solution)/shard_map/pallas_call | solution.py:45
  200.6 1.7 convolution_subtract_fusion.1
  202.3 1.8 convolution_subtract_fusion.8
  204.7 15.0 %shard_map.69 = f32[128,128]{1,0:T(8,128)} custom-call(f32[128,128]{1,0:T(8,128)} %slice.174.a_ref), custom_call_target="tpu_custom_call" | custom-call | tf_op jit(solution)/shard_map/pallas_call | solution.py:45
  223.4 1.6 convolution_subtract_fusion.9
  225.7 15.0 %shard_map.70 = f32[128,128]{1,0:T(8,128)} custom-call(f32[128,128]{1,0:T(8,128)} %slice.179.a_ref), custom_call_target="tpu_custom_call" | custom-call | tf_op jit(solution)/shard_map/pallas_call | solution.py:45
  243.0 1.7 convolution_subtract_fusion.6.a_ref
  246.3 15.0 %shard_map.71 = f32[128,128]{1,0:T(8,128)} custom-call(f32[128,128]{1,0:T(8,128)} %convolution_subtract_fusion.6.a_ref), custom_call_target="tpu_custom_call" | custom-call | tf_op jit(solution)/shard_map/pallas_call | solution.py:45
  275.5 4.6 %shard_map.72 = f32[32,32]{1,0:T(8,128)} custom-call(f32[32,32]{1,0:T(8,128)} %convolution_add_fusion.a_ref), custom_call_target="tpu_custom_call" | custom-call | tf_op jit(solution)/shard_map/pallas_call | solution.py:45
  282.1 2.0 convolution_multiply_fusion.1
  (138 shorter events, 52.2 us)
Async XLA Ops:
  7.4 3.4 %copy-start.26 = (bf16[2048,32]{0,1:T(8,128)(2,1)S(1)}, bf16[2048,32]{0,1:T(8,128)(2,1)}, u32[]{:S(2)}) copy-start(bf16[2048,32]{0,1:T(8,128)(2,1)} %param.8) | copy-start | bytes 393220
  7.4 5.5 %copy-start.27 = (bf16[16,1024]{1,0:T(8,128)(2,1)S(1)}, bf16[16,1024]{1,0:T(8,128)(2,1)}, u32[]{:S(2)}) copy-start(bf16[16,1024]{1,0:T(8,128)(2,1)} %param.11) | copy-start | bytes 98308
  7.4 39.9 %all-reduce.4.cloned.1.call-start = ((), (), s32[]{:S(2)}) async-start(), calls=%async_computation | async-start | bytes 262144 | tf_op jit(solution)/shard_map/psum | solution.py:130
  9.0 1.8 copy-start.10
  12.2 69.2 %all-gather.3.cloned.1.call-start = ((), (), s32[]{:S(2)}) async-start(), calls=%async_computation.1 | async-start | bytes 4325376 | tf_op jit(solution)/shard_map/all_gather | solution.py:118
  12.8 160.7 %all-reduce.6.cloned.1.call-start = ((), (), s32[]{:S(2)}) async-start(), calls=%async_computation.2 | async-start | bytes 1310720 | tf_op jit(solution)/shard_map/psum | solution.py:111
  12.9 35.6 %copy-start.9 = (f32[128,1024]{1,0:T(8,128)}, f32[128,1024]{1,0:T(8,128)S(1)}, u32[]{:S(2)}) copy-start(f32[128,1024]{1,0:T(8,128)S(1)} %convert_dynamic-update-slice_fusion) | copy-start | bytes 1572868
  87.3 2.0 copy-start.1
  173.5 6.9 %copy-start.5 = (f32[640,640]{1,0:T(8,128)S(1)}, f32[640,640]{1,0:T(8,128)}, u32[]{:S(2)}) copy-start(f32[640,640]{1,0:T(8,128)} %copy-done.4) | copy-start | bytes 4915204
  177.3 2.0 copy-start.20
  180.4 2.0 copy-start.22
  199.4 2.9 copy-start.6
  200.5 3.6 %copy-start.23 = (f32[128,32]{0,1:T(8,128)}, f32[128,32]{0,1:T(8,128)S(1)}, u32[]{:S(2)}) copy-start(f32[128,32]{0,1:T(8,128)S(1)} %fusion.41) | copy-start | bytes 49156
  202.3 1.8 copy-start.11
  220.9 2.5 copy-start.8
  222.0 3.0 %copy-start.25 = (f32[128,32]{0,1:T(8,128)}, f32[128,32]{0,1:T(8,128)S(1)}, u32[]{:S(2)}) copy-start(f32[128,32]{0,1:T(8,128)S(1)} %fusion.39) | copy-start | bytes 49156
  223.4 1.7 copy-start.15
  241.9 2.9 copy-start.12
  243.0 1.8 copy-start.24
  261.3 12.0 %copy-start.21 = (f32[128,32]{0,1:T(8,128)S(1)}, f32[128,32]{0,1:T(8,128)}, u32[]{:S(2)}) copy-start(f32[128,32]{0,1:T(8,128)} %copy-done.20) | copy-start | bytes 49156
  261.3 12.4 %copy-start.13 = (f32[128,128]{1,0:T(8,128)S(1)}, f32[128,128]{1,0:T(8,128)}, u32[]{:S(2)}) copy-start(f32[128,128]{1,0:T(8,128)} %shard_map.65) | copy-start | bytes 196612
  261.3 12.6 %copy-start.19 = (f32[32,128]{1,0:T(8,128)S(1)}, f32[32,128]{1,0:T(8,128)}, u32[]{:S(2)}) copy-start(f32[32,128]{1,0:T(8,128)} %copy-done.18) | copy-start | bytes 49156
  261.3 13.0 %copy-start.14 = (f32[128,128]{1,0:T(8,128)S(1)}, f32[128,128]{1,0:T(8,128)}, u32[]{:S(2)}) copy-start(f32[128,128]{1,0:T(8,128)} %shard_map.64) | copy-start | bytes 196612
  261.3 13.3 %copy-start.17 = (f32[32,1024]{1,0:T(8,128)S(1)}, f32[32,1024]{1,0:T(8,128)}, u32[]{:S(2)}) copy-start(f32[32,1024]{1,0:T(8,128)} %get-tuple-element.6) | copy-start | bytes 393220
  (7 other events, 9.1 us)
Sparse Core Ops, SparseCore 0:
  12.3 34.9 all-reduce.3
  51.2 80.2 all-reduce.5
Sparse Core Ops, SparseCore 1:
  15.6 65.8 all-gather.2
where the time goes:
time: 294 us; the launch traced here: 291 us
  Pallas kernels  125 us (43%)
  waiting for transfers between devices  67.2 us (23%)
  matrix products  63.7 us (22%)
  local copies, waits for them, and re-layouts  19.2 us (7%)
  between operations  15.7 us (5%)
    pallas_call x9, Pallas kernels, inverse_factor(): pl.pallas_call(_inverse_factor_kernel, out_shape=jax.ShapeDtypeStruct((n,...  125 us
    dot_general x47, matrix products, mm(): jnp.dot(a, b, precision=lax.Precision.HIGHEST, preferred_element_type=jnp...  59.2 us
    psum x1, waiting for transfers between devices, per_device(): factors = lax.psum(factors, 'param')  34.4 us
    all_gather x1, waiting for transfers between devices, gather_prior(): blocks = lax.all_gather(prior, ('ex', 'param'), axis=0, tiled=False)  32.2 us
    unnamed x75, local copies, waits for them, and re-layouts  9.72 us
  transfers between devices with their start and end apart: 3, of which 2 were waited for; matrix products, arithmetic and copies ran while one was open for 9% of the time, Pallas kernels for 21%

commit v1 on v0

--- a/solution.py
+++ b/solution.py
@@ -6,6 +6,11 @@
 from jax.experimental import pallas as pl
 from jax.experimental.pallas import tpu as pltpu
 from jax.sharding import PartitionSpec as P
+
+
+def _pick(row, index):
+    lane = lax.broadcasted_iota(jnp.int32, row.shape, 1)
+    return jnp.sum(jnp.where(lane == index, row, 0.0), axis=1, keepdims=True)
 
 
 def _inverse_factor_kernel(a_ref, w_ref, s_ref):
@@ -18,26 +23,38 @@
         low = group * 8
 
         def step(t, carry):
-            j = low + t
-            pivot_row = s_ref[pl.ds(j, 1), :]
-            inverse_row = w_ref[pl.ds(j, 1), :]
-            lane = lax.broadcasted_iota(jnp.int32, (1, n), 1)
-            pivot = jnp.sum(jnp.where(lane == j, pivot_row, 0.0), axis=1, keepdims=True)
-            scale = 1.0 / jnp.sqrt(pivot)
-            pivot_row = pivot_row * scale
-            inverse_row = inverse_row * scale
+            j = low + 2 * t
+            first = s_ref[pl.ds(j, 1), :]
+            second = s_ref[pl.ds(j + 1, 1), :]
+            first_inv = w_ref[pl.ds(j, 1), :]
+            second_inv = w_ref[pl.ds(j + 1, 1), :]
+            lead = _pick(first, j)
+            cross = _pick(first, j + 1)
+            tail = _pick(second, j + 1)
+            scale0 = 1.0 / jnp.sqrt(lead)
+            ratio = cross / lead
+            scale1 = 1.0 / jnp.sqrt(tail - cross * ratio)
+            second = (second - ratio * first) * scale1
+            second_inv = (second_inv - ratio * first_inv) * scale1
+            first = first * scale0
+            first_inv = first_inv * scale0
             rest = s_ref[low:, :]
             lanes = lax.broadcasted_iota(jnp.int32, rest.shape, 1)
-            column = jnp.sum(jnp.where(lanes == j, rest, 0.0), axis=1, keepdims=True)
+            col0 = jnp.sum(jnp.where(lanes == j, rest, 0.0), axis=1, keepdims=True)
+            col1 = jnp.sum(jnp.where(lanes == j + 1, rest, 0.0), axis=1, keepdims=True)
             below = lax.broadcasted_iota(jnp.int32, (n - low, 1), 0) + low
-            factor = jnp.where(below > j, column * scale, 0.0)
-            s_ref[low:, :] = rest - factor * pivot_row
-            w_ref[low:, :] = w_ref[low:, :] - factor * inverse_row
-            s_ref[pl.ds(j, 1), :] = pivot_row
-            w_ref[pl.ds(j, 1), :] = inverse_row
+            keep = below > j + 1
+            factor0 = jnp.where(keep, col0 * scale0, 0.0)
+            factor1 = jnp.where(keep, (col1 - col0 * ratio) * scale1, 0.0)
+            s_ref[low:, :] = rest - factor0 * first - factor1 * second
+            w_ref[low:, :] = w_ref[low:, :] - factor0 * first_inv - factor1 * second_inv
+            s_ref[pl.ds(j, 1), :] = first
+            s_ref[pl.ds(j + 1, 1), :] = second
+            w_ref[pl.ds(j, 1), :] = first_inv
+            w_ref[pl.ds(j + 1, 1), :] = second_inv
             return carry
 
-        lax.fori_loop(0, 8, step, 0)
+        lax.fori_loop(0, 4, step, 0)
 
 
 def inverse_factor(block):

time: 294 us -> 245 us (0.83)
  Pallas kernels: 125 us -> 75.8 us
    pallas_call x9, Pallas kernels: 125 us -> 75.8 us  [inverse_factor(): pl.pallas_call(_inverse_factor_kernel, out_shape=jax.ShapeDtypeStruct((n,...]
  transfers between devices with their start and end apart: 3 -> 3, of which waited for: 2 -> 2; matrix products, arithmetic and copies ran while one was open for 9% -> 11% of each run, Pallas kernels for 21% -> 15%
where the time goes in v1:
time: 245 us; the launch traced here: 242 us
  Pallas kernels  75.8 us (31%)
  waiting for transfers between devices  67.2 us (27%)
  matrix products  63.7 us (26%)
  local copies, waits for them, and re-layouts  19.2 us (8%)
  between operations  15.7 us (6%)
    pallas_call x9, Pallas kernels, inverse_factor(): pl.pallas_call(_inverse_factor_kernel, out_shape=jax.ShapeDtypeStruct((n,...  75.8 us
    dot_general x47, matrix products, mm(): jnp.dot(a, b, precision=lax.Precision.HIGHEST, preferred_element_type=jnp...  59.3 us
    psum x1, waiting for transfers between devices, per_device(): factors = lax.psum(factors, 'param')  34.4 us
    all_gather x1, waiting for transfers between devices, gather_prior(): blocks = lax.all_gather(prior, ('ex', 'param'), axis=0, tiled=False)  32.2 us
    unnamed x75, local copies, waits for them, and re-layouts  9.72 us
  transfers between devices with their start and end apart: 3, of which 2 were waited for; matrix products, arithmetic and copies ran while one was open for 11% of the time, Pallas kernels for 15%

profile of v1, /device:TPU:0, one launch (start us, length us, event | category | flops | bytes accessed | tf_op | source)
XLA Modules:
  0.0 242.4 jit_solution(8400143760492864927)
XLA Ops:
  7.4 1.6 copy-done
  9.0 1.8 convolution_bitcast_fusion
  12.9 34.4 %all-reduce.4.cloned.1.call-done = f32[4,64,128]{2,1,0:T(8,128)} async-done(((f32[4,64,128]{2,1,0:T(8,128)}), f32[4,64,128]{2,1,0:T(8,128)}) %all-reduce.4.cloned.1.call-update) | async-done | bytes 131088 | tf_op jit(solution)/shard_map/psum | solution.py:147
  49.2 32.2 %all-gather.3.cloned.1.call-done = f32[4096,256]{1,0:T(8,128)} async-done(((f32[128,256]{1,0:T(8,128)}), f32[4096,256]{1,0:T(8,128)}) %all-gather.3.cloned.1.call-update) | async-done | bytes 4194320 | tf_op jit(solution)/shard_map/all_gather | solution.py:135
  81.4 4.9 %copy.7 = f32[8,4,128,256]{3,1,2,0:T(4,128)S(1)} copy(f32[8,4,128,256]{3,2,1,0:T(8,128)} %bitcast.106) | data formatting | bytes 8388608 | tf_op jit(solution)/shard_map/reshape | solution.py:136
  87.4 2.0 copy-done.1
  89.9 9.2 %shard_map.64 = f32[128,128]{1,0:T(8,128)} custom-call(f32[128,128]{1,0:T(8,128)} %slice.151.a_ref), custom_call_target="tpu_custom_call" | custom-call | tf_op jit(solution)/shard_map/pallas_call | solution.py:62
  100.7 4.8 %slice_subtract_fusion = f32[896,896]{1,0:T(8,128)S(1)} fusion(f32[1024,1024]{1,0:T(8,128)} %bitcast.105, f32[896,128]{1,0:T(8,128)S(1)} %fusion.3), kind=kOutput, calls=%fused_computation | convolution fusion | flops 1233928192 | bytes 7340032 | tf_op jit(solution)/shard_map/dot_general | solution.py:87
  105.5 1.6 copy-done.2
  107.8 9.0 %shard_map.65 = f32[128,128]{1,0:T(8,128)} custom-call(f32[128,128]{1,0:T(8,128)} %slice.154.a_ref), custom_call_target="tpu_custom_call" | custom-call | tf_op jit(solution)/shard_map/pallas_call | solution.py:62
  118.3 3.7 %slice_subtract_fusion.1 = f32[768,768]{1,0:T(8,128)S(1)} fusion(f32[896,896]{1,0:T(8,128)} %copy-done.2, f32[768,128]{1,0:T(8,128)S(1)} %fusion.5), kind=kOutput, calls=%fused_computation.1 | convolution fusion | flops 906559488 | bytes 5505024 | tf_op jit(solution)/shard_map/dot_general | solution.py:87
  124.1 9.0 %shard_map.66 = f32[128,128]{1,0:T(8,128)} custom-call(f32[128,128]{1,0:T(8,128)} %slice.159.a_ref), custom_call_target="tpu_custom_call" | custom-call | tf_op jit(solution)/shard_map/pallas_call | solution.py:62
  134.6 2.9 %slice_subtract_fusion.2 = f32[640,640]{1,0:T(8,128)S(1)} fusion(f32[768,768]{1,0:T(8,128)} %copy-done.3, f32[640,128]{1,0:T(8,128)S(1)} %fusion.7), kind=kOutput, calls=%fused_computation.2 | convolution fusion | flops 629555200 | bytes 3932160 | tf_op jit(solution)/shard_map/dot_general | solution.py:87
  139.3 9.2 %shard_map.67 = f32[128,128]{1,0:T(8,128)} custom-call(f32[128,128]{1,0:T(8,128)} %slice.164.a_ref), custom_call_target="tpu_custom_call" | custom-call | tf_op jit(solution)/shard_map/pallas_call | solution.py:62
  159.5 9.0 %shard_map.68 = f32[128,128]{1,0:T(8,128)} custom-call(f32[128,128]{1,0:T(8,128)} %slice.169.a_ref), custom_call_target="tpu_custom_call" | custom-call | tf_op jit(solution)/shard_map/pallas_call | solution.py:62
  170.9 1.7 convolution_subtract_fusion.1
  172.7 1.8 convolution_subtract_fusion.8
  175.1 9.0 %shard_map.69 = f32[128,128]{1,0:T(8,128)} custom-call(f32[128,128]{1,0:T(8,128)} %slice.174.a_ref), custom_call_target="tpu_custom_call" | custom-call | tf_op jit(solution)/shard_map/pallas_call | solution.py:62
  187.8 1.6 convolution_subtract_fusion.9
  190.1 9.0 %shard_map.70 = f32[128,128]{1,0:T(8,128)} custom-call(f32[128,128]{1,0:T(8,128)} %slice.179.a_ref), custom_call_target="tpu_custom_call" | custom-call | tf_op jit(solution)/shard_map/pallas_call | solution.py:62
  201.4 1.7 convolution_subtract_fusion.6.a_ref
  204.6 9.0 %shard_map.71 = f32[128,128]{1,0:T(8,128)} custom-call(f32[128,128]{1,0:T(8,128)} %convolution_subtract_fusion.6.a_ref), custom_call_target="tpu_custom_call" | custom-call | tf_op jit(solution)/shard_map/pallas_call | solution.py:62
  227.8 3.1 %shard_map.72 = f32[32,32]{1,0:T(8,128)} custom-call(f32[32,32]{1,0:T(8,128)} %convolution_add_fusion.a_ref), custom_call_target="tpu_custom_call" | custom-call | tf_op jit(solution)/shard_map/pallas_call | solution.py:62
  232.9 2.0 convolution_multiply_fusion.1
  (138 shorter events, 52.2 us)
Async XLA Ops:
  7.4 3.4 %copy-start.26 = (bf16[2048,32]{0,1:T(8,128)(2,1)S(1)}, bf16[2048,32]{0,1:T(8,128)(2,1)}, u32[]{:S(2)}) copy-start(bf16[2048,32]{0,1:T(8,128)(2,1)} %param.8) | copy-start | bytes 393220
  7.4 5.5 %copy-start.27 = (bf16[16,1024]{1,0:T(8,128)(2,1)S(1)}, bf16[16,1024]{1,0:T(8,128)(2,1)}, u32[]{:S(2)}) copy-start(bf16[16,1024]{1,0:T(8,128)(2,1)} %param.11) | copy-start | bytes 98308
  7.4 39.9 %all-reduce.4.cloned.1.call-start = ((), (), s32[]{:S(2)}) async-start(), calls=%async_computation | async-start | bytes 262144 | tf_op jit(solution)/shard_map/psum | solution.py:147
  9.0 1.8 copy-start.10
  12.2 69.2 %all-gather.3.cloned.1.call-start = ((), (), s32[]{:S(2)}) async-start(), calls=%async_computation.1 | async-start | bytes 4325376 | tf_op jit(solution)/shard_map/all_gather | solution.py:135
  12.8 137.1 %all-reduce.6.cloned.1.call-start = ((), (), s32[]{:S(2)}) async-start(), calls=%async_computation.2 | async-start | bytes 1310720 | tf_op jit(solution)/shard_map/psum | solution.py:128
  12.9 35.6 %copy-start.9 = (f32[128,1024]{1,0:T(8,128)}, f32[128,1024]{1,0:T(8,128)S(1)}, u32[]{:S(2)}) copy-start(f32[128,1024]{1,0:T(8,128)S(1)} %convert_dynamic-update-slice_fusion) | copy-start | bytes 1572868
  87.3 2.0 copy-start.1
  149.9 6.9 %copy-start.5 = (f32[640,640]{1,0:T(8,128)S(1)}, f32[640,640]{1,0:T(8,128)}, u32[]{:S(2)}) copy-start(f32[640,640]{1,0:T(8,128)} %copy-done.4) | copy-start | bytes 4915204
  153.6 2.0 copy-start.20
  156.8 2.0 copy-start.22
  169.8 2.9 %copy-start.6 = (f32[384,128]{1,0:T(8,128)}, f32[384,128]{1,0:T(8,128)S(1)}, u32[]{:S(2)}) copy-start(f32[384,128]{1,0:T(8,128)S(1)} %fusion.11) | copy-start | bytes 589828
  170.9 3.6 %copy-start.23 = (f32[128,32]{0,1:T(8,128)}, f32[128,32]{0,1:T(8,128)S(1)}, u32[]{:S(2)}) copy-start(f32[128,32]{0,1:T(8,128)S(1)} %fusion.41) | copy-start | bytes 49156
  172.6 1.8 copy-start.11
  185.3 2.5 %copy-start.8 = (f32[256,128]{1,0:T(8,128)}, f32[256,128]{1,0:T(8,128)S(1)}, u32[]{:S(2)}) copy-start(f32[256,128]{1,0:T(8,128)S(1)} %fusion.13) | copy-start | bytes 393220
  186.4 3.0 %copy-start.25 = (f32[128,32]{0,1:T(8,128)}, f32[128,32]{0,1:T(8,128)S(1)}, u32[]{:S(2)}) copy-start(f32[128,32]{0,1:T(8,128)S(1)} %fusion.39) | copy-start | bytes 49156
  187.8 1.7 copy-start.15
  200.3 2.9 %copy-start.12 = (f32[128,128]{1,0:T(8,128)}, f32[128,128]{1,0:T(8,128)S(1)}, u32[]{:S(2)}) copy-start(f32[128,128]{1,0:T(8,128)S(1)} %fusion.17) | copy-start | bytes 196612
  201.3 1.8 copy-start.24
  213.7 12.0 %copy-start.21 = (f32[128,32]{0,1:T(8,128)S(1)}, f32[128,32]{0,1:T(8,128)}, u32[]{:S(2)}) copy-start(f32[128,32]{0,1:T(8,128)} %copy-done.20) | copy-start | bytes 49156
  213.7 12.4 %copy-start.13 = (f32[128,128]{1,0:T(8,128)S(1)}, f32[128,128]{1,0:T(8,128)}, u32[]{:S(2)}) copy-start(f32[128,128]{1,0:T(8,128)} %shard_map.65) | copy-start | bytes 196612
  213.7 12.6 %copy-start.19 = (f32[32,128]{1,0:T(8,128)S(1)}, f32[32,128]{1,0:T(8,128)}, u32[]{:S(2)}) copy-start(f32[32,128]{1,0:T(8,128)} %copy-done.18) | copy-start | bytes 49156
  213.7 13.0 %copy-start.14 = (f32[128,128]{1,0:T(8,128)S(1)}, f32[128,128]{1,0:T(8,128)}, u32[]{:S(2)}) copy-start(f32[128,128]{1,0:T(8,128)} %shard_map.64) | copy-start | bytes 196612
  213.7 13.3 %copy-start.17 = (f32[32,1024]{1,0:T(8,128)S(1)}, f32[32,1024]{1,0:T(8,128)}, u32[]{:S(2)}) copy-start(f32[32,1024]{1,0:T(8,128)} %get-tuple-element.6) | copy-start | bytes 393220
  (7 other events, 9.1 us)
Sparse Core Ops, SparseCore 0:
  12.3 34.9 all-reduce.3
  51.2 80.1 all-reduce.5
Sparse Core Ops, SparseCore 1:
  15.6 65.8 all-gather.2

commit v2 on v0

--- a/solution.py
+++ b/solution.py
@@ -1,3 +1,4 @@
+import functools
 import math
 
 import jax
@@ -8,42 +9,76 @@
 from jax.sharding import PartitionSpec as P
 
 
-def _inverse_factor_kernel(a_ref, w_ref, s_ref):
+def _pick(row, index):
+    lane = lax.broadcasted_iota(jnp.int32, row.shape, 1)
+    return jnp.sum(jnp.where(lane == index, row, 0.0), axis=1, keepdims=True)
+
+
+def _inverse_factor_kernel(width, a_ref, w_ref, s_ref):
     n = a_ref.shape[0]
     s_ref[...] = a_ref[...]
     rows = lax.broadcasted_iota(jnp.int32, (n, n), 0)
     cols = lax.broadcasted_iota(jnp.int32, (n, n), 1)
     w_ref[...] = jnp.where(rows == cols, 1.0, 0.0).astype(jnp.float32)
-    for group in range(n // 8):
-        low = group * 8
+    segment = 32 if n % 32 == 0 else 8
+    for group in range(n // segment):
+        low = group * segment
 
         def step(t, carry):
-            j = low + t
-            pivot_row = s_ref[pl.ds(j, 1), :]
-            inverse_row = w_ref[pl.ds(j, 1), :]
-            lane = lax.broadcasted_iota(jnp.int32, (1, n), 1)
-            pivot = jnp.sum(jnp.where(lane == j, pivot_row, 0.0), axis=1, keepdims=True)
-            scale = 1.0 / jnp.sqrt(pivot)
-            pivot_row = pivot_row * scale
-            inverse_row = inverse_row * scale
+            j = low + width * t
+            pivots = [s_ref[pl.ds(j + m, 1), :] for m in range(width)]
+            inverses = [w_ref[pl.ds(j + m, 1), :] for m in range(width)]
+            block = [[None] * width for _ in range(width)]
+            for m in range(width):
+                for l in range(m + 1):
+                    block[m][l] = _pick(pivots[m], j + l)
+                    block[l][m] = block[m][l]
+            coeffs = [[1.0 if l == m else 0.0 for l in range(width)] for m in range(width)]
+            for m in range(width):
+                scale = 1.0 / jnp.sqrt(block[m][m])
+                block[m] = [b * scale for b in block[m]]
+                coeffs[m] = [c * scale for c in coeffs[m]]
+                for q in range(m + 1, width):
+                    factor = block[q][m] * scale
+                    block[q] = [bq - factor * bm for bq, bm in zip(block[q], block[m])]
+                    coeffs[q] = [cq - factor * cm for cq, cm in zip(coeffs[q], coeffs[m])]
+            new_pivots, new_inverses = [], []
+            for m in range(width):
+                p = pivots[0] * coeffs[m][0]
+                v = inverses[0] * coeffs[m][0]
+                for l in range(1, m + 1):
+                    p = p + pivots[l] * coeffs[m][l]
+                    v = v + inverses[l] * coeffs[m][l]
+                new_pivots.append(p)
+                new_inverses.append(v)
             rest = s_ref[low:, :]
             lanes = lax.broadcasted_iota(jnp.int32, rest.shape, 1)
-            column = jnp.sum(jnp.where(lanes == j, rest, 0.0), axis=1, keepdims=True)
+            columns = [jnp.sum(jnp.where(lanes == j + l, rest, 0.0), axis=1, keepdims=True) for l in range(width)]
             below = lax.broadcasted_iota(jnp.int32, (n - low, 1), 0) + low
-            factor = jnp.where(below > j, column * scale, 0.0)
-            s_ref[low:, :] = rest - factor * pivot_row
-            w_ref[low:, :] = w_ref[low:, :] - factor * inverse_row
-            s_ref[pl.ds(j, 1), :] = pivot_row
-            w_ref[pl.ds(j, 1), :] = inverse_row
+            keep = below >= j + width
+            new_rest = rest
+            new_inv = w_ref[low:, :]
+            for m in range(width):
+                f = columns[0] * coeffs[m][0]
+                for l in range(1, m + 1):
+                    f = f + columns[l] * coeffs[m][l]
+                f = jnp.where(keep, f, 0.0)
+                new_rest = new_rest - f * new_pivots[m]
+                new_inv = new_inv - f * new_inverses[m]
+            s_ref[low:, :] = new_rest
+            w_ref[low:, :] = new_inv
+            for m in range(width):
+                s_ref[pl.ds(j + m, 1), :] = new_pivots[m]
+                w_ref[pl.ds(j + m, 1), :] = new_inverses[m]
             return carry
 
-        lax.fori_loop(0, 8, step, 0)
-
-
-def inverse_factor(block):
+        lax.fori_loop(0, segment // width, step, 0)
+
+
+def inverse_factor(block, width=4):
     n = block.shape[0]
     return pl.pallas_call(
-        _inverse_factor_kernel,
+        functools.partial(_inverse_factor_kernel, width),
         out_shape=jax.ShapeDtypeStruct((n, n), jnp.float32),
         in_specs=[pl.BlockSpec(memory_space=pltpu.VMEM)],
         out_specs=pl.BlockSpec(memory_space=pltpu.VMEM),

time: 294 us -> 229 us (0.78)
  Pallas kernels: 125 us -> 60.6 us
    pallas_call x9, Pallas kernels: 125 us -> 60.6 us  [inverse_factor(): pl.pallas_call(functools.partial(_inverse_factor_kernel, width), out_shap...]
  transfers between devices with their start and end apart: 3 -> 3, of which waited for: 2 -> 2; matrix products, arithmetic and copies ran while one was open for 9% -> 12% of each run, Pallas kernels for 21% -> 13%
where the time goes in v2:
time: 229 us; the launch traced here: 227 us
  waiting for transfers between devices  67.2 us (29%)
  matrix products  63.7 us (28%)
  Pallas kernels  60.6 us (26%)
  local copies, waits for them, and re-layouts  19.2 us (8%)
  between operations  15.7 us (7%)
    pallas_call x9, Pallas kernels, inverse_factor(): pl.pallas_call(functools.partial(_inverse_factor_kernel, width), out_shap...  60.6 us
    dot_general x47, matrix products, mm(): jnp.dot(a, b, precision=lax.Precision.HIGHEST, preferred_element_type=jnp...  59.3 us
    psum x1, waiting for transfers between devices, per_device(): factors = lax.psum(factors, 'param')  34.4 us
    all_gather x1, waiting for transfers between devices, gather_prior(): blocks = lax.all_gather(prior, ('ex', 'param'), axis=0, tiled=False)  32.2 us
    unnamed x75, local copies, waits for them, and re-layouts  9.72 us
    reshape x1, local copies, waits for them, and re-layouts, gather_prior(): blocks = blocks.reshape(n_ex, n_par, rows, cols).transpose(0, 2, 1, 3)  4.89 us
  transfers between devices with their start and end apart: 3, of which 2 were waited for; matrix products, arithmetic and copies ran while one was open for 12% of the time, Pallas kernels for 13%

profile of v2, /device:TPU:0, one launch (start us, length us, event | category | flops | bytes accessed | tf_op | source)
XLA Modules:
  0.0 227.2 jit_solution(6171602118366876343)
XLA Ops:
  7.4 1.6 copy-done
  9.0 1.8 convolution_bitcast_fusion
  12.9 34.4 %all-reduce.4.cloned.1.call-done = f32[4,64,128]{2,1,0:T(8,128)} async-done(((f32[4,64,128]{2,1,0:T(8,128)}), f32[4,64,128]{2,1,0:T(8,128)}) %all-reduce.4.cloned.1.call-update) | async-done | bytes 131088 | tf_op jit(solution)/shard_map/psum | solution.py:165
  49.2 32.2 %all-gather.3.cloned.1.call-done = f32[4096,256]{1,0:T(8,128)} async-done(((f32[128,256]{1,0:T(8,128)}), f32[4096,256]{1,0:T(8,128)}) %all-gather.3.cloned.1.call-update) | async-done | bytes 4194320 | tf_op jit(solution)/shard_map/all_gather | solution.py:153
  81.4 4.9 %copy.7 = f32[8,4,128,256]{3,1,2,0:T(4,128)S(1)} copy(f32[8,4,128,256]{3,2,1,0:T(8,128)} %bitcast.106) | data formatting | bytes 8388608 | tf_op jit(solution)/shard_map/reshape | solution.py:154
  87.4 2.0 copy-done.1
  89.9 7.4 %shard_map.64 = f32[128,128]{1,0:T(8,128)} custom-call(f32[128,128]{1,0:T(8,128)} %slice.151.a_ref), custom_call_target="tpu_custom_call" | custom-call | tf_op jit(solution)/shard_map/pallas_call | solution.py:80
  98.9 4.8 %slice_subtract_fusion = f32[896,896]{1,0:T(8,128)S(1)} fusion(f32[1024,1024]{1,0:T(8,128)} %bitcast.105, f32[896,128]{1,0:T(8,128)S(1)} %fusion.3), kind=kOutput, calls=%fused_computation | convolution fusion | flops 1233928192 | bytes 7340032 | tf_op jit(solution)/shard_map/dot_general | solution.py:105
  103.8 1.6 copy-done.2
  106.0 7.2 %shard_map.65 = f32[128,128]{1,0:T(8,128)} custom-call(f32[128,128]{1,0:T(8,128)} %slice.154.a_ref), custom_call_target="tpu_custom_call" | custom-call | tf_op jit(solution)/shard_map/pallas_call | solution.py:80
  114.7 3.7 %slice_subtract_fusion.1 = f32[768,768]{1,0:T(8,128)S(1)} fusion(f32[896,896]{1,0:T(8,128)} %copy-done.2, f32[768,128]{1,0:T(8,128)S(1)} %fusion.5), kind=kOutput, calls=%fused_computation.1 | convolution fusion | flops 906559488 | bytes 5505024 | tf_op jit(solution)/shard_map/dot_general | solution.py:105
  120.5 7.2 %shard_map.66 = f32[128,128]{1,0:T(8,128)} custom-call(f32[128,128]{1,0:T(8,128)} %slice.159.a_ref), custom_call_target="tpu_custom_call" | custom-call | tf_op jit(solution)/shard_map/pallas_call | solution.py:80
  129.1 2.9 %slice_subtract_fusion.2 = f32[640,640]{1,0:T(8,128)S(1)} fusion(f32[768,768]{1,0:T(8,128)} %copy-done.3, f32[640,128]{1,0:T(8,128)S(1)} %fusion.7), kind=kOutput, calls=%fused_computation.2 | convolution fusion | flops 629555200 | bytes 3932160 | tf_op jit(solution)/shard_map/dot_general | solution.py:105
  133.8 7.2 %shard_map.67 = f32[128,128]{1,0:T(8,128)} custom-call(f32[128,128]{1,0:T(8,128)} %slice.164.a_ref), custom_call_target="tpu_custom_call" | custom-call | tf_op jit(solution)/shard_map/pallas_call | solution.py:80
  152.0 7.2 %shard_map.68 = f32[128,128]{1,0:T(8,128)} custom-call(f32[128,128]{1,0:T(8,128)} %slice.169.a_ref), custom_call_target="tpu_custom_call" | custom-call | tf_op jit(solution)/shard_map/pallas_call | solution.py:80
  161.6 1.7 convolution_subtract_fusion.1
  163.4 1.8 convolution_subtract_fusion.8
  165.8 7.2 %shard_map.69 = f32[128,128]{1,0:T(8,128)} custom-call(f32[128,128]{1,0:T(8,128)} %slice.174.a_ref), custom_call_target="tpu_custom_call" | custom-call | tf_op jit(solution)/shard_map/pallas_call | solution.py:80
  176.7 1.6 convolution_subtract_fusion.9
  179.0 7.2 %shard_map.70 = f32[128,128]{1,0:T(8,128)} custom-call(f32[128,128]{1,0:T(8,128)} %slice.179.a_ref), custom_call_target="tpu_custom_call" | custom-call | tf_op jit(solution)/shard_map/pallas_call | solution.py:80
  188.5 1.7 convolution_subtract_fusion.6.a_ref
  191.8 7.2 %shard_map.71 = f32[128,128]{1,0:T(8,128)} custom-call(f32[128,128]{1,0:T(8,128)} %convolution_subtract_fusion.6.a_ref), custom_call_target="tpu_custom_call" | custom-call | tf_op jit(solution)/shard_map/pallas_call | solution.py:80
  213.1 2.6 %shard_map.72 = f32[32,32]{1,0:T(8,128)} custom-call(f32[32,32]{1,0:T(8,128)} %convolution_add_fusion.a_ref), custom_call_target="tpu_custom_call" | custom-call | tf_op jit(solution)/shard_map/pallas_call | solution.py:80
  217.8 2.0 convolution_multiply_fusion.1
  (138 shorter events, 52.2 us)
Async XLA Ops:
  7.4 3.4 %copy-start.26 = (bf16[2048,32]{0,1:T(8,128)(2,1)S(1)}, bf16[2048,32]{0,1:T(8,128)(2,1)}, u32[]{:S(2)}) copy-start(bf16[2048,32]{0,1:T(8,128)(2,1)} %param.8) | copy-start | bytes 393220
  7.4 5.5 %copy-start.27 = (bf16[16,1024]{1,0:T(8,128)(2,1)S(1)}, bf16[16,1024]{1,0:T(8,128)(2,1)}, u32[]{:S(2)}) copy-start(bf16[16,1024]{1,0:T(8,128)(2,1)} %param.11) | copy-start | bytes 98308
  7.4 39.9 %all-reduce.4.cloned.1.call-start = ((), (), s32[]{:S(2)}) async-start(), calls=%async_computation | async-start | bytes 262144 | tf_op jit(solution)/shard_map/psum | solution.py:165
  9.0 1.8 copy-start.10
  12.2 69.2 %all-gather.3.cloned.1.call-start = ((), (), s32[]{:S(2)}) async-start(), calls=%async_computation.1 | async-start | bytes 4325376 | tf_op jit(solution)/shard_map/all_gather | solution.py:153
  12.8 129.6 %all-reduce.6.cloned.1.call-start = ((), (), s32[]{:S(2)}) async-start(), calls=%async_computation.2 | async-start | bytes 1310720 | tf_op jit(solution)/shard_map/psum | solution.py:146
  12.9 35.6 %copy-start.9 = (f32[128,1024]{1,0:T(8,128)}, f32[128,1024]{1,0:T(8,128)S(1)}, u32[]{:S(2)}) copy-start(f32[128,1024]{1,0:T(8,128)S(1)} %convert_dynamic-update-slice_fusion) | copy-start | bytes 1572868
  87.3 2.0 copy-start.1
  142.4 6.9 %copy-start.5 = (f32[640,640]{1,0:T(8,128)S(1)}, f32[640,640]{1,0:T(8,128)}, u32[]{:S(2)}) copy-start(f32[640,640]{1,0:T(8,128)} %copy-done.4) | copy-start | bytes 4915204
  146.2 2.1 copy-start.20
  149.3 2.0 copy-start.22
  160.5 2.9 %copy-start.6 = (f32[384,128]{1,0:T(8,128)}, f32[384,128]{1,0:T(8,128)S(1)}, u32[]{:S(2)}) copy-start(f32[384,128]{1,0:T(8,128)S(1)} %fusion.11) | copy-start | bytes 589828
  161.6 3.6 %copy-start.23 = (f32[128,32]{0,1:T(8,128)}, f32[128,32]{0,1:T(8,128)S(1)}, u32[]{:S(2)}) copy-start(f32[128,32]{0,1:T(8,128)S(1)} %fusion.41) | copy-start | bytes 49156
  163.4 1.8 copy-start.11
  174.2 2.5 %copy-start.8 = (f32[256,128]{1,0:T(8,128)}, f32[256,128]{1,0:T(8,128)S(1)}, u32[]{:S(2)}) copy-start(f32[256,128]{1,0:T(8,128)S(1)} %fusion.13) | copy-start | bytes 393220
  175.3 3.0 %copy-start.25 = (f32[128,32]{0,1:T(8,128)}, f32[128,32]{0,1:T(8,128)S(1)}, u32[]{:S(2)}) copy-start(f32[128,32]{0,1:T(8,128)S(1)} %fusion.39) | copy-start | bytes 49156
  176.7 1.7 copy-start.15
  187.4 2.9 %copy-start.12 = (f32[128,128]{1,0:T(8,128)}, f32[128,128]{1,0:T(8,128)S(1)}, u32[]{:S(2)}) copy-start(f32[128,128]{1,0:T(8,128)S(1)} %fusion.17) | copy-start | bytes 196612
  188.4 1.8 copy-start.24
  199.0 12.0 %copy-start.21 = (f32[128,32]{0,1:T(8,128)S(1)}, f32[128,32]{0,1:T(8,128)}, u32[]{:S(2)}) copy-start(f32[128,32]{0,1:T(8,128)} %copy-done.20) | copy-start | bytes 49156
  199.0 12.4 %copy-start.13 = (f32[128,128]{1,0:T(8,128)S(1)}, f32[128,128]{1,0:T(8,128)}, u32[]{:S(2)}) copy-start(f32[128,128]{1,0:T(8,128)} %shard_map.65) | copy-start | bytes 196612
  199.0 12.6 %copy-start.19 = (f32[32,128]{1,0:T(8,128)S(1)}, f32[32,128]{1,0:T(8,128)}, u32[]{:S(2)}) copy-start(f32[32,128]{1,0:T(8,128)} %copy-done.18) | copy-start | bytes 49156
  199.0 13.0 %copy-start.14 = (f32[128,128]{1,0:T(8,128)S(1)}, f32[128,128]{1,0:T(8,128)}, u32[]{:S(2)}) copy-start(f32[128,128]{1,0:T(8,128)} %shard_map.64) | copy-start | bytes 196612
  199.0 13.3 %copy-start.17 = (f32[32,1024]{1,0:T(8,128)S(1)}, f32[32,1024]{1,0:T(8,128)}, u32[]{:S(2)}) copy-start(f32[32,1024]{1,0:T(8,128)} %get-tuple-element.6) | copy-start | bytes 393220
  (7 other events, 9.1 us)
Sparse Core Ops, SparseCore 0:
  12.3 34.9 all-reduce.3
  51.2 80.0 all-reduce.5
Sparse Core Ops, SparseCore 1:
  15.6 65.8 all-gather.2

commit v3 on v2

--- a/solution.py
+++ b/solution.py
@@ -105,36 +105,21 @@
     return jnp.dot(a, b, precision=lax.Precision.HIGHEST, preferred_element_type=jnp.float32)
 
 
-def blocked_cholesky(matrix, block):
+def block_eliminate(matrix, rhs, block):
     count = matrix.shape[0] // block
-    inverses, panels = [], []
-    trailing = matrix
+    trailing = jnp.concatenate((matrix, rhs), axis=1)
+    tops = []
     for k in range(count):
         inverse = inverse_factor(trailing[:block, :block])
-        inverses.append(inverse)
+        top = mm(inverse.T, mm(inverse, trailing[:block, block:]))
+        tops.append(top)
         if k + 1 < count:
-            panel = mm(trailing[block:, :block], inverse.T)
-            panels.append(panel)
-            trailing = trailing[block:, block:] - mm(panel, panel.T)
-    return inverses, panels
-
-
-def blocked_solve(inverses, panels, rhs, block):
-    count = len(inverses)
-    parts = []
-    rest = rhs
-    for k in range(count):
-        part = mm(inverses[k], rest[:block])
-        parts.append(part)
-        if k + 1 < count:
-            rest = rest[block:] - mm(panels[k], part)
-    done = None
-    for k in reversed(range(count)):
-        target = parts[k]
-        if done is not None:
-            target = target - mm(panels[k].T, done)
-        part = mm(inverses[k].T, target)
-        done = part if done is None else jnp.concatenate((part, done), axis=0)
+            trailing = trailing[block:, block:] - mm(trailing[block:, :block], top)
+    done = tops[-1]
+    for k in reversed(range(count - 1)):
+        width = done.shape[0]
+        part = tops[k][:, width:] - mm(tops[k][:, :width], done)
+        done = jnp.concatenate((part, done), axis=0)
     return done
 
 
@@ -169,8 +154,7 @@
     all_features = gather_rows(features.astype(jnp.float32), "ex")
     train_count = all_features.shape[0]
     block = 128 if feat_dim % 128 == 0 else feat_dim
-    inverses, panels = blocked_cholesky(full_prior, block)
-    prior_solved_t = blocked_solve(inverses, panels, all_features.T, block)
+    prior_solved_t = block_eliminate(full_prior, all_features.T, block)
     gram = jnp.dot(all_features, prior_solved_t, precision=lax.Precision.HIGHEST)
     small = gram + train_count * jnp.eye(train_count, dtype=jnp.float32)
     small_inverse = inverse_factor(small)
@@ -179,7 +163,7 @@
     row_start = lax.axis_index("ex") * local_count
     solved = lax.dynamic_slice_in_dim(solved_all, row_start, local_count, 0)
     inverse_root = 1.0 / math.sqrt(feat_dim)
-    block_probes = gather_rows(probes.astype(jnp.float32), "ex")
+    block_probes = gather_rows(probes.astype(jnp.float32) + 0.0 * all_features[:1, :1], "ex")
     return mm(block_probes, solved.astype(jnp.float32).T) * inverse_root
 
 

time: 229 us -> 282 us (1.23)
  waiting for transfers between devices: 67.2 us -> 112 us
  local copies, waits for them, and re-layouts: 19.2 us -> 31.3 us
  matrix products: 63.7 us -> 59.5 us
    psum x1 -> x2, waiting for transfers between devices: 0.02 us -> 77.5 us  [gather_rows(): return lax.psum(padded, axis_name)]
    all_gather x1, waiting for transfers between devices: 32.2 us -> 0.03 us  [gather_prior(): blocks = lax.all_gather(prior, ('ex', 'param'), axis=0, tiled=False)]
    unnamed x75 -> x57, local copies, waits for them, and re-layouts: 9.72 us -> 17.5 us
    dot_general x47 -> x33, matrix products: 59.3 us -> 52.8 us  [mm(): jnp.dot(a, b, precision=lax.Precision.HIGHEST, preferred_element_type=jnp...]
    slice x7 -> x9, local copies, waits for them, and re-layouts: 4.42 us -> 6.2 us  [the longest x8 5.02 us: block_eliminate(): inverse = inverse_factor(trailing[:block, :block])]
  transfers between devices with their start and end apart: 3 -> 4, of which waited for: 2 -> 2; matrix products, arithmetic and copies ran while one was open for 12% -> 23% of each run, Pallas kernels for 13% -> 22%
where the time goes in v3:
time: 282 us; the launch traced here: 280 us
  waiting for transfers between devices  112 us (40%)
  Pallas kernels  60.5 us (21%)
  matrix products  59.5 us (21%)
  local copies, waits for them, and re-layouts  31.3 us (11%)
  between operations  15.8 us (6%)
    psum x2, waiting for transfers between devices, gather_rows(): return lax.psum(padded, axis_name)  77.5 us
    pallas_call x9, Pallas kernels, inverse_factor(): pl.pallas_call(functools.partial(_inverse_factor_kernel, width), out_shap...  60.5 us
    dot_general x33, matrix products, mm(): jnp.dot(a, b, precision=lax.Precision.HIGHEST, preferred_element_type=jnp...  52.8 us
    psum x1, waiting for transfers between devices, per_device(): factors = lax.psum(factors, 'param')  34.2 us
    unnamed x57, local copies, waits for them, and re-layouts  17.5 us
  transfers between devices with their start and end apart: 4, of which 2 were waited for; matrix products, arithmetic and copies ran while one was open for 23% of the time, Pallas kernels for 22%

profile of v3, /device:TPU:0, one launch (start us, length us, event | category | flops | bytes accessed | tf_op | source)
XLA Modules:
  0.0 280.2 jit_solution(16532634676179108832)
XLA Ops:
  10.6 2.4 convolution_bitcast_fusion
  13.8 34.2 %all-reduce.4.cloned.1.call-done = f32[4,64,128]{2,1,0:T(8,128)} async-done(((f32[4,64,128]{2,1,0:T(8,128)}), f32[4,64,128]{2,1,0:T(8,128)}) %all-reduce.4.cloned.1.call-update) | async-done | bytes 131088 | tf_op jit(solution)/shard_map/psum | solution.py:150
  49.4 2.3 dynamic_update_slice.6
  53.1 77.4 %all-reduce.6.cloned.1.call-done = f32[32,1024]{0,1:T(8,128)} async-done(((f32[32,1024]{0,1:T(8,128)}), f32[32,1024]{0,1:T(8,128)}) %all-reduce.6.cloned.1.call-update) | async-done | bytes 131088 | tf_op jit(solution)/shard_map/psum | solution.py:131
  133.4 4.9 %copy.8 = f32[8,4,128,256]{3,1,2,0:T(4,128)S(1)} copy(f32[8,4,128,256]{3,2,1,0:T(8,128)} %bitcast.71) | data formatting | bytes 8388608 | tf_op jit(solution)/shard_map/reshape | solution.py:139
  139.3 1.9 copy-done.1
  141.8 7.4 %shard_map.64 = f32[128,128]{1,0:T(8,128)} custom-call(f32[128,128]{1,0:T(8,128)} %slice.191.a_ref), custom_call_target="tpu_custom_call" | custom-call | tf_op jit(solution)/shard_map/pallas_call | solution.py:80
  149.2 2.0 fusion.4
  151.8 5.3 %fusion = f32[896,928]{1,0:T(8,128)S(1)} fusion(f32[1024,32]{1,0:T(8,128)S(1)} %bitcast.70, f32[1024,1024]{1,0:T(8,128)} %bitcast.67, f32[928,128]{1,0:T(8,128)S(1)} %fusion.64), kind=kOutput, calls=%fused_computation.1 | convolution fusion | flops 1278828544 | bytes 8585216 | tf_op jit(solution)/shard_map/dot_general | solution.py:105
  157.1 1.8 copy-done.2
  159.5 7.2 %shard_map.65 = f32[128,128]{1,0:T(8,128)} custom-call(f32[128,128]{1,0:T(8,128)} %slice.195.a_ref), custom_call_target="tpu_custom_call" | custom-call | tf_op jit(solution)/shard_map/pallas_call | solution.py:80
  168.3 1.7 fusion.65
  170.1 4.4 %slice_subtract_fusion = f32[768,800]{1,0:T(8,128)S(1)} fusion(f32[896,928]{1,0:T(8,128)} %copy-done.2, f32[128,800]{0,1:T(8,128)S(1)} %fusion.65), kind=kOutput, calls=%fused_computation.2 | convolution fusion | flops 944332800 | bytes 6012928 | tf_op jit(solution)/shard_map/dot_general | solution.py:105
  176.6 7.2 %shard_map.66 = f32[128,128]{1,0:T(8,128)} custom-call(f32[128,128]{1,0:T(8,128)} %slice.201.a_ref), custom_call_target="tpu_custom_call" | custom-call | tf_op jit(solution)/shard_map/pallas_call | solution.py:80
  187.7 3.4 %slice_subtract_fusion.1 = f32[640,672]{1,0:T(8,128)S(1)} fusion(f32[768,800]{1,0:T(8,128)} %copy-done.4, f32[128,672]{0,1:T(8,128)S(1)} %fusion.66), kind=kOutput, calls=%fused_computation.3 | convolution fusion | flops 661032960 | bytes 4358144 | tf_op jit(solution)/shard_map/dot_general | solution.py:105
  193.0 7.2 %shard_map.67 = f32[128,128]{1,0:T(8,128)} custom-call(f32[128,128]{1,0:T(8,128)} %slice.207.a_ref), custom_call_target="tpu_custom_call" | custom-call | tf_op jit(solution)/shard_map/pallas_call | solution.py:80
  203.9 2.6 convolution_subtract_fusion
  208.2 7.2 %shard_map.68 = f32[128,128]{1,0:T(8,128)} custom-call(f32[128,128]{1,0:T(8,128)} %slice.213.a_ref), custom_call_target="tpu_custom_call" | custom-call | tf_op jit(solution)/shard_map/pallas_call | solution.py:80
  218.9 2.1 convolution_subtract_fusion.1
  222.5 7.2 %shard_map.69 = f32[128,128]{1,0:T(8,128)} custom-call(f32[128,128]{1,0:T(8,128)} %slice.219.a_ref), custom_call_target="tpu_custom_call" | custom-call | tf_op jit(solution)/shard_map/pallas_call | solution.py:80
  235.8 7.2 %shard_map.70 = f32[128,128]{1,0:T(8,128)} custom-call(f32[128,128]{1,0:T(8,128)} %slice.225.a_ref), custom_call_target="tpu_custom_call" | custom-call | tf_op jit(solution)/shard_map/pallas_call | solution.py:80
  248.7 7.2 %shard_map.71 = f32[128,128]{1,0:T(8,128)} custom-call(f32[128,128]{1,0:T(8,128)} %slice.231.a_ref), custom_call_target="tpu_custom_call" | custom-call | tf_op jit(solution)/shard_map/pallas_call | solution.py:80
  266.5 2.6 shard_map.72
  271.1 2.0 convolution_multiply_fusion.1
  (111 shorter events, 55.5 us)
Async XLA Ops:
  7.4 1.6 copy-start
  7.4 40.6 %all-reduce.4.cloned.1.call-start = ((), (), s32[]{:S(2)}) async-start(), calls=%async_computation | async-start | bytes 262144 | tf_op jit(solution)/shard_map/psum | solution.py:150
  10.6 121.9 %copy-start.18 = (bf16[16,1024]{1,0:T(8,128)(2,1)S(1)}, bf16[16,1024]{1,0:T(8,128)(2,1)}, u32[]{:S(2)}) copy-start(bf16[16,1024]{1,0:T(8,128)(2,1)} %param.11) | copy-start | bytes 98308
  13.7 116.9 %all-reduce.6.cloned.1.call-start = ((), (), s32[]{:S(2)}) async-start(), calls=%async_computation.1 | async-start | bytes 1048576 | tf_op jit(solution)/shard_map/psum | solution.py:131
  51.7 0.8 copy-start.10
  52.5 80.8 %all-gather.3.cloned.1.call-start = ((), (), s32[]{:S(2)}) async-start(), calls=%async_computation.3 | async-start | bytes 4325376 | tf_op jit(solution)/shard_map/all_gather | solution.py:138
  53.1 218.0 %all-reduce.8.cloned.1.call-start = ((), (), s32[]{:S(2)}) async-start(), calls=%async_computation.2 | async-start | bytes 1048576 | tf_op jit(solution)/shard_map/psum | solution.py:131
  132.5 0.8 copy-start.9
  138.2 11.0 %copy-start.3 = (f32[32,1024]{0,1:T(8,128)S(1)}, f32[32,1024]{0,1:T(8,128)}, u32[]{:S(2)}) copy-start(f32[32,1024]{0,1:T(8,128)} %all-reduce.6.cloned.1.call-done) | copy-start | bytes 393220
  139.3 1.9 copy-start.1
  149.2 2.0 copy-start.16
  157.1 1.8 copy-start.2
  174.4 1.5 copy-start.4
  187.0 0.7 copy-start.6
  191.1 1.3 copy-start.5
  203.2 0.7 copy-start.8
  206.5 1.1 copy-start.7
  218.2 0.7 copy-start.11
  221.0 0.9 copy-start.12
  232.3 0.7 copy-start.13
  234.5 0.7 copy-start.14
  245.5 0.6 copy-start.15
  247.4 0.7 copy-start.17
Sparse Core Ops, SparseCore 0:
  13.8 34.0 all-reduce.3
  52.6 77.9 all-reduce.5
  134.0 71.6 all-reduce.7
Sparse Core Ops, SparseCore 1:
  56.3 63.2 all-gather.2

commit v4 on v2

--- a/solution.py
+++ b/solution.py
@@ -151,8 +151,9 @@
     n_par = lax.axis_size("param")
     rows, cols = prior.shape
     blocks = lax.all_gather(prior, ("ex", "param"), axis=0, tiled=False)
-    blocks = blocks.reshape(n_ex, n_par, rows, cols).transpose(0, 2, 1, 3)
-    return blocks.reshape(n_ex * rows, n_par * cols)
+    return jnp.concatenate(
+        [jnp.concatenate([blocks[e * n_par + p] for p in range(n_par)], axis=1) for e in range(n_ex)], axis=0
+    )
 
 
 def per_device(activations, out_grads, proj_in, proj_out, prior, probes):

time: 229 us -> 265 us (1.16)
  waiting for transfers between devices: 67.2 us -> 108 us
  local copies, waits for them, and re-layouts: 19.2 us -> 12.7 us
    psum x1, waiting for transfers between devices: 0.02 us -> 41.3 us  [gather_rows(): return lax.psum(padded, axis_name)]
    reshape x1 -> x0, local copies, waits for them, and re-layouts: 4.89 us -> none  [gather_prior(): blocks = blocks.reshape(n_ex, n_par, rows, cols).transpose(0, 2, 1, 3)]
    unnamed x75 -> x72, local copies, waits for them, and re-layouts: 9.72 us -> 5.62 us
  transfers between devices with their start and end apart: 3 -> 3, of which waited for: 2 -> 3; matrix products, arithmetic and copies ran while one was open for 12% -> 1% of each run, Pallas kernels for 13% -> 3%
where the time goes in v4:
time: 265 us; the launch traced here: 262 us
  waiting for transfers between devices  108 us (41%)
  matrix products  63.9 us (24%)
  Pallas kernels  60.4 us (23%)
  between operations  15.7 us (6%)
  local copies, waits for them, and re-layouts  12.7 us (5%)
    pallas_call x9, Pallas kernels, inverse_factor(): pl.pallas_call(functools.partial(_inverse_factor_kernel, width), out_shap...  60.4 us
    dot_general x47, matrix products, mm(): jnp.dot(a, b, precision=lax.Precision.HIGHEST, preferred_element_type=jnp...  57.9 us
    psum x1, waiting for transfers between devices, gather_rows(): return lax.psum(padded, axis_name)  41.3 us
    psum x1, waiting for transfers between devices, per_device(): factors = lax.psum(factors, 'param')  34.4 us
    all_gather x1, waiting for transfers between devices, gather_prior(): blocks = lax.all_gather(prior, ('ex', 'param'), axis=0, tiled=False)  32.2 us
    unnamed x72, local copies, waits for them, and re-layouts  5.62 us
  transfers between devices with their start and end apart: 3, of which 3 were waited for; matrix products, arithmetic and copies ran while one was open for 1% of the time, Pallas kernels for 3%

profile of v4, /device:TPU:0, one launch (start us, length us, event | category | flops | bytes accessed | tf_op | source)
XLA Modules:
  0.0 262.3 jit_solution(12628707966292763077)
XLA Ops:
  7.4 1.6 copy-done
  9.0 1.6 convolution_bitcast_fusion.1
  10.6 2.4 convolution_bitcast_fusion
  14.4 34.4 %all-reduce.4.cloned.1.call-done = f32[4,64,128]{2,1,0:T(8,128)} async-done(((f32[4,64,128]{2,1,0:T(8,128)}), f32[4,64,128]{2,1,0:T(8,128)}) %all-reduce.4.cloned.1.call-update) | async-done | bytes 131088 | tf_op jit(solution)/shard_map/psum | solution.py:166
  50.7 32.2 %all-gather.3.cloned.1.call-done = f32[4096,256]{1,0:T(8,128)} async-done(((f32[128,256]{1,0:T(8,128)}), f32[4096,256]{1,0:T(8,128)}) %all-gather.3.cloned.1.call-update) | async-done | bytes 4194320 | tf_op jit(solution)/shard_map/all_gather | solution.py:153
  84.4 7.2 %shard_map.64 = f32[128,128]{1,0:T(8,128)} custom-call(f32[128,128]{1,0:T(8,128)} %slice.302.a_ref), custom_call_target="tpu_custom_call" | custom-call | tf_op jit(solution)/shard_map/pallas_call | solution.py:80
  91.6 41.3 %all-reduce.6.cloned.1.call-done = (f32[128,1024]{1,0:T(8,128)}, f32[32,1024]{1,0:T(8,128)}) async-done(((f32[128,1024]{1,0:T(8,128)}, f32[32,1024]{1,0:T(8,128)}), (f32[128,1024]{1,0:T(8,128)}, f32[32,1024]{1,0:T(8,128)})) %all-reduce.6.cloned.1.call-update) | async-done | bytes 655376 | tf_op jit(solution)/shard_map/psum | solution.py:146
  137.4 2.9 %slice_subtract_fusion = f32[896,896]{1,0:T(8,128)S(1)} fusion(f32[896,1024]{1,0:T(8,128)S(1)} %maximum_dynamic-update-slice_fusion, f32[896,128]{1,0:T(8,128)S(1)} %fusion.3), kind=kOutput, calls=%fused_computation | convolution fusion | flops 1233928192 | bytes 7340032 | tf_op jit(solution)/shard_map/dot_general | solution.py:105
  140.2 1.6 copy-done.1
  142.5 7.2 %shard_map.65 = f32[128,128]{1,0:T(8,128)} custom-call(f32[128,128]{1,0:T(8,128)} %slice.333.a_ref), custom_call_target="tpu_custom_call" | custom-call | tf_op jit(solution)/shard_map/pallas_call | solution.py:80
  152.9 3.7 %slice_subtract_fusion.1 = f32[768,768]{1,0:T(8,128)S(1)} fusion(f32[896,896]{1,0:T(8,128)} %copy-done.1, f32[768,128]{1,0:T(8,128)S(1)} %fusion.5), kind=kOutput, calls=%fused_computation.1 | convolution fusion | flops 906559488 | bytes 5505024 | tf_op jit(solution)/shard_map/dot_general | solution.py:105
  158.6 7.2 %shard_map.66 = f32[128,128]{1,0:T(8,128)} custom-call(f32[128,128]{1,0:T(8,128)} %slice.338.a_ref), custom_call_target="tpu_custom_call" | custom-call | tf_op jit(solution)/shard_map/pallas_call | solution.py:80
  168.3 2.9 %slice_subtract_fusion.2 = f32[640,640]{1,0:T(8,128)S(1)} fusion(f32[768,768]{1,0:T(8,128)} %copy-done.2, f32[640,128]{1,0:T(8,128)S(1)} %fusion.7), kind=kOutput, calls=%fused_computation.2 | convolution fusion | flops 629555200 | bytes 3932160 | tf_op jit(solution)/shard_map/dot_general | solution.py:105
  173.0 7.2 %shard_map.67 = f32[128,128]{1,0:T(8,128)} custom-call(f32[128,128]{1,0:T(8,128)} %slice.343.a_ref), custom_call_target="tpu_custom_call" | custom-call | tf_op jit(solution)/shard_map/pallas_call | solution.py:80
  182.7 2.3 convolution_subtract_fusion
  186.6 7.2 %shard_map.68 = f32[128,128]{1,0:T(8,128)} custom-call(f32[128,128]{1,0:T(8,128)} %slice.348.a_ref), custom_call_target="tpu_custom_call" | custom-call | tf_op jit(solution)/shard_map/pallas_call | solution.py:80
  196.3 1.7 convolution_subtract_fusion.1
  198.0 1.8 convolution_subtract_fusion.8
  200.4 7.2 %shard_map.69 = f32[128,128]{1,0:T(8,128)} custom-call(f32[128,128]{1,0:T(8,128)} %slice.353.a_ref), custom_call_target="tpu_custom_call" | custom-call | tf_op jit(solution)/shard_map/pallas_call | solution.py:80
  211.3 1.6 convolution_subtract_fusion.9
  213.6 7.2 %shard_map.70 = f32[128,128]{1,0:T(8,128)} custom-call(f32[128,128]{1,0:T(8,128)} %slice.358.a_ref), custom_call_target="tpu_custom_call" | custom-call | tf_op jit(solution)/shard_map/pallas_call | solution.py:80
  223.1 1.7 convolution_subtract_fusion.6.a_ref
  226.3 7.2 %shard_map.71 = f32[128,128]{1,0:T(8,128)} custom-call(f32[128,128]{1,0:T(8,128)} %convolution_subtract_fusion.6.a_ref), custom_call_target="tpu_custom_call" | custom-call | tf_op jit(solution)/shard_map/pallas_call | solution.py:80
  249.3 2.6 shard_map.72
  (143 shorter events, 52.5 us)
Async XLA Ops:
  7.4 7.0 %copy-start.26 = (bf16[16,1024]{1,0:T(8,128)(2,1)S(1)}, bf16[16,1024]{1,0:T(8,128)(2,1)}, u32[]{:S(2)}) copy-start(bf16[16,1024]{1,0:T(8,128)(2,1)} %param.11) | copy-start | bytes 98308
  7.4 41.4 %all-reduce.4.cloned.1.call-start = ((), (), s32[]{:S(2)}) async-start(), calls=%async_computation | async-start | bytes 262144 | tf_op jit(solution)/shard_map/psum | solution.py:166
  13.7 69.2 %all-gather.3.cloned.1.call-start = ((), (), s32[]{:S(2)}) async-start(), calls=%async_computation.1 | async-start | bytes 4325376 | tf_op jit(solution)/shard_map/all_gather | solution.py:153
  14.3 118.7 %all-reduce.6.cloned.1.call-start = ((), (), s32[]{:S(2)}) async-start(), calls=%async_computation.2 | async-start | bytes 1310720 | tf_op jit(solution)/shard_map/psum | solution.py:146
  14.4 35.6 %copy-start.8 = (f32[128,1024]{1,0:T(8,128)}, f32[128,1024]{1,0:T(8,128)S(1)}, u32[]{:S(2)}) copy-start(f32[128,1024]{1,0:T(8,128)S(1)} %convert_dynamic-update-slice_fusion) | copy-start | bytes 1572868
  132.9 2.9 %copy-start.6 = (f32[4096,256]{1,0:T(8,128)S(1)}, f32[4096,256]{1,0:T(8,128)}, u32[]{:S(2)}) copy-start(f32[4096,256]{1,0:T(8,128)} %all-gather.3.cloned.1.call-done) | copy-start | bytes 12582916
  134.1 15.6 %copy-start.19 = (f32[32,128]{1,0:T(8,128)}, f32[32,128]{1,0:T(8,128)S(1)}, u32[]{:S(2)}) copy-start(f32[32,128]{1,0:T(8,128)S(1)} %fusion.49) | copy-start | bytes 49156
  137.3 12.4 %copy-start.16 = (f32[32,1024]{1,0:T(8,128)S(1)}, f32[32,1024]{1,0:T(8,128)}, u32[]{:S(2)}) copy-start(f32[32,1024]{1,0:T(8,128)} %get-tuple-element.6) | copy-start | bytes 393220
  140.2 1.7 copy-start.1
  152.8 5.8 %copy-start.21 = (f32[128,32]{0,1:T(8,128)}, f32[128,32]{0,1:T(8,128)S(1)}, u32[]{:S(2)}) copy-start(f32[128,32]{0,1:T(8,128)S(1)} %fusion.47) | copy-start | bytes 49156
  180.2 4.7 %copy-start.18 = (f32[640,32]{0,1:T(8,128)S(1)}, f32[640,32]{0,1:T(8,128)}, u32[]{:S(2)}) copy-start(f32[640,32]{0,1:T(8,128)} %convolution_subtract_fusion.5) | copy-start | bytes 245764
  182.6 3.3 %copy-start.22 = (f32[128,32]{0,1:T(8,128)}, f32[128,32]{0,1:T(8,128)S(1)}, u32[]{:S(2)}) copy-start(f32[128,32]{0,1:T(8,128)S(1)} %fusion.43) | copy-start | bytes 49156
  195.1 2.9 %copy-start.4 = (f32[384,128]{1,0:T(8,128)}, f32[384,128]{1,0:T(8,128)S(1)}, u32[]{:S(2)}) copy-start(f32[384,128]{1,0:T(8,128)S(1)} %fusion.11) | copy-start | bytes 589828
  196.2 3.6 %copy-start.23 = (f32[128,32]{0,1:T(8,128)}, f32[128,32]{0,1:T(8,128)S(1)}, u32[]{:S(2)}) copy-start(f32[128,32]{0,1:T(8,128)S(1)} %fusion.41) | copy-start | bytes 49156
  198.0 1.8 copy-start.9
  208.9 2.5 copy-start.7
  210.0 3.0 %copy-start.25 = (f32[128,32]{0,1:T(8,128)}, f32[128,32]{0,1:T(8,128)S(1)}, u32[]{:S(2)}) copy-start(f32[128,32]{0,1:T(8,128)S(1)} %fusion.39) | copy-start | bytes 49156
  211.3 1.6 copy-start.13
  221.9 2.8 %copy-start.10 = (f32[128,128]{1,0:T(8,128)}, f32[128,128]{1,0:T(8,128)S(1)}, u32[]{:S(2)}) copy-start(f32[128,128]{1,0:T(8,128)S(1)} %fusion.17) | copy-start | bytes 196612
  223.0 1.8 copy-start.24
  233.6 14.2 %copy-start.20 = (f32[32,128]{1,0:T(8,128)S(1)}, f32[32,128]{1,0:T(8,128)}, u32[]{:S(2)}) copy-start(f32[32,128]{1,0:T(8,128)} %copy-done.19) | copy-start | bytes 49156
  233.6 14.6 %copy-start.12 = (f32[128,128]{1,0:T(8,128)S(1)}, f32[128,128]{1,0:T(8,128)}, u32[]{:S(2)}) copy-start(f32[128,128]{1,0:T(8,128)} %shard_map.64) | copy-start | bytes 196612
  233.6 14.8 %copy-start.17 = (f32[32,1024]{1,0:T(8,128)S(1)}, f32[32,1024]{1,0:T(8,128)}, u32[]{:S(2)}) copy-start(f32[32,1024]{1,0:T(8,128)} %get-tuple-element.6) | copy-start | bytes 393220
  244.5 9.4 %copy-start.15 = (f32[128,1024]{1,0:T(8,128)S(1)}, f32[128,1024]{1,0:T(8,128)}, u32[]{:S(2)}) copy-start(f32[128,1024]{1,0:T(8,128)} %get-tuple-element.5) | copy-start | bytes 1572868
  (6 other events, 6.7 us)
Sparse Core Ops, SparseCore 0:
  13.8 34.9 all-reduce.3
  52.6 80.2 all-reduce.5
Sparse Core Ops, SparseCore 1:
  17.0 65.8 all-gather.2

commit v5 on v4

--- a/solution.py
+++ b/solution.py
@@ -167,7 +167,9 @@
     summed = outer_terms(factors, in_width)
     features = (summed * (1.0 / math.sqrt(tokens))).astype(jnp.bfloat16)
     local_count, feat_dim = features.shape
-    all_features = gather_rows(features.astype(jnp.float32), "ex")
+    everyone = lax.all_gather(features.astype(jnp.float32), ("ex", "param"), axis=0, tiled=False)
+    all_features = everyone.reshape(lax.axis_size("ex"), lax.axis_size("param"), local_count, feat_dim)[:, 0]
+    all_features = all_features.reshape(-1, feat_dim)
     train_count = all_features.shape[0]
     block = 128 if feat_dim % 128 == 0 else feat_dim
     inverses, panels = blocked_cholesky(full_prior, block)

time: 265 us -> 234 us (0.88)
  waiting for transfers between devices: 108 us -> 34.1 us
  blocking collectives: 0 us -> 42.6 us
    all_gather x0 -> x1, blocking collectives: none -> 42.6 us  [per_device(): lax.all_gather(features.astype(jnp.float32), ('ex', 'param'), axis=0, til...]
    psum x1, waiting for transfers between devices: 41.3 us -> 0.02 us  [gather_rows(): return lax.psum(padded, axis_name)]
    all_gather x1, waiting for transfers between devices: 32.2 us -> 0.03 us  [gather_prior(): blocks = lax.all_gather(prior, ('ex', 'param'), axis=0, tiled=False)]
    unnamed x72 -> x69, local copies, waits for them, and re-layouts: 5.62 us -> 5.79 us
  transfers between devices with their start and end apart: 3 -> 3, of which waited for: 3 -> 1; matrix products, arithmetic and copies ran while one was open for 1% -> 29% of each run, Pallas kernels for 3% -> 26%
where the time goes in v5:
time: 234 us; the launch traced here: 232 us
  matrix products  64.9 us (28%)
  Pallas kernels  60.4 us (26%)
  blocking collectives  42.6 us (18%)
  waiting for transfers between devices  34.1 us (15%)
  between operations  15.7 us (7%)
  local copies, waits for them, and re-layouts  12.9 us (6%)
    pallas_call x9, Pallas kernels, inverse_factor(): pl.pallas_call(functools.partial(_inverse_factor_kernel, width), out_shap...  60.4 us
    dot_general x47, matrix products, mm(): jnp.dot(a, b, precision=lax.Precision.HIGHEST, preferred_element_type=jnp...  58.9 us
    all_gather x1, blocking collectives, per_device(): lax.all_gather(features.astype(jnp.float32), ('ex', 'param'), axis=0, til...  42.6 us
    psum x1, waiting for transfers between devices, per_device(): factors = lax.psum(factors, 'param')  33.5 us
    unnamed x69, local copies, waits for them, and re-layouts  5.79 us
    slice x7, local copies, waits for them, and re-layouts, blocked_cholesky(): inverse = inverse_factor(trailing[:block, :block])  5.24 us
  transfers between devices with their start and end apart: 3, of which 1 were waited for; matrix products, arithmetic and copies ran while one was open for 29% of the time, Pallas kernels for 26%

profile of v5, /device:TPU:0, one launch (start us, length us, event | category | flops | bytes accessed | tf_op | source)
XLA Modules:
  0.0 231.8 jit_solution(16054950073004745474)
XLA Ops:
  7.4 1.6 copy-done
  9.0 1.6 convolution_bitcast_fusion.1
  10.6 2.4 %convolution_bitcast_fusion = f32[4,32,128]{2,1,0:T(8,128)S(1)} fusion(bf16[4,128,2048]{2,1,0:T(8,128)(2,1)} %param.7, bf16[2048,32]{0,1:T(8,128)(2,1)} %param.9), kind=kOutput, calls=%fused_computation.12 | convolution fusion | flops 67108864 | bytes 2293760 | tf_op jit(solution)/shard_map/eld,dk->ekl/dot_general | solution.py:164
  15.2 33.5 %all-reduce.5.cloned.1.call-done = f32[4,64,128]{2,1,0:T(8,128)} async-done(((f32[4,64,128]{2,1,0:T(8,128)}), f32[4,64,128]{2,1,0:T(8,128)}) %all-reduce.5.cloned.1.call-update) | async-done | bytes 131088 | tf_op jit(solution)/shard_map/psum | solution.py:166
  50.0 42.6 %all_gather.10 = f32[32,4,1024]{2,1,0:T(4,128)S(1)} all-gather(f32[1,4,1024]{2,1,0:T(4,128)S(1)} %reshape.26), channel_id=1, replica_groups=mesh['param'=4,'ex'=8] {'ex','param'}, dimensions={0}, use_global_device_ids=true | all-gather | bytes 540672 | tf_op jit(solution)/shard_map/all_gather | solution.py:170
  94.2 7.2 %shard_map.64 = f32[128,128]{1,0:T(8,128)} custom-call(f32[128,128]{1,0:T(8,128)} %slice.307.a_ref), custom_call_target="tpu_custom_call" | custom-call | tf_op jit(solution)/shard_map/pallas_call | solution.py:80
  105.9 2.8 %slice_subtract_fusion = f32[896,896]{1,0:T(8,128)S(1)} fusion(f32[896,1024]{1,0:T(8,128)S(1)} %maximum_dynamic-update-slice_fusion, f32[896,128]{1,0:T(8,128)S(1)} %fusion.3), kind=kOutput, calls=%fused_computation | convolution fusion | flops 1233928192 | bytes 7340032 | tf_op jit(solution)/shard_map/dot_general | solution.py:105
  108.7 1.6 copy-done.1
  111.0 7.2 %shard_map.65 = f32[128,128]{1,0:T(8,128)} custom-call(f32[128,128]{1,0:T(8,128)} %slice.338.a_ref), custom_call_target="tpu_custom_call" | custom-call | tf_op jit(solution)/shard_map/pallas_call | solution.py:80
  121.4 3.7 %slice_subtract_fusion.1 = f32[768,768]{1,0:T(8,128)S(1)} fusion(f32[896,896]{1,0:T(8,128)} %copy-done.1, f32[768,128]{1,0:T(8,128)S(1)} %fusion.5), kind=kOutput, calls=%fused_computation.1 | convolution fusion | flops 906559488 | bytes 5505024 | tf_op jit(solution)/shard_map/dot_general | solution.py:105
  127.1 7.2 %shard_map.66 = f32[128,128]{1,0:T(8,128)} custom-call(f32[128,128]{1,0:T(8,128)} %slice.343.a_ref), custom_call_target="tpu_custom_call" | custom-call | tf_op jit(solution)/shard_map/pallas_call | solution.py:80
  136.8 2.9 %slice_subtract_fusion.2 = f32[640,640]{1,0:T(8,128)S(1)} fusion(f32[768,768]{1,0:T(8,128)} %copy-done.2, f32[640,128]{1,0:T(8,128)S(1)} %fusion.7), kind=kOutput, calls=%fused_computation.2 | convolution fusion | flops 629555200 | bytes 3932160 | tf_op jit(solution)/shard_map/dot_general | solution.py:105
  141.5 7.2 %shard_map.67 = f32[128,128]{1,0:T(8,128)} custom-call(f32[128,128]{1,0:T(8,128)} %slice.348.a_ref), custom_call_target="tpu_custom_call" | custom-call | tf_op jit(solution)/shard_map/pallas_call | solution.py:80
  151.2 2.3 convolution_subtract_fusion
  155.1 7.2 %shard_map.68 = f32[128,128]{1,0:T(8,128)} custom-call(f32[128,128]{1,0:T(8,128)} %slice.353.a_ref), custom_call_target="tpu_custom_call" | custom-call | tf_op jit(solution)/shard_map/pallas_call | solution.py:80
  164.8 1.7 convolution_subtract_fusion.1
  166.5 1.8 convolution_subtract_fusion.8
  168.9 7.2 %shard_map.69 = f32[128,128]{1,0:T(8,128)} custom-call(f32[128,128]{1,0:T(8,128)} %slice.358.a_ref), custom_call_target="tpu_custom_call" | custom-call | tf_op jit(solution)/shard_map/pallas_call | solution.py:80
  179.8 1.6 convolution_subtract_fusion.9
  182.1 7.2 %shard_map.70 = f32[128,128]{1,0:T(8,128)} custom-call(f32[128,128]{1,0:T(8,128)} %slice.363.a_ref), custom_call_target="tpu_custom_call" | custom-call | tf_op jit(solution)/shard_map/pallas_call | solution.py:80
  191.6 1.7 convolution_subtract_fusion.6.a_ref
  194.8 7.2 %shard_map.71 = f32[128,128]{1,0:T(8,128)} custom-call(f32[128,128]{1,0:T(8,128)} %convolution_subtract_fusion.6.a_ref), custom_call_target="tpu_custom_call" | custom-call | tf_op jit(solution)/shard_map/pallas_call | solution.py:80
  217.7 2.6 %shard_map.72 = f32[32,32]{1,0:T(8,128)} custom-call(f32[32,32]{1,0:T(8,128)} %convolution_add_fusion.a_ref), custom_call_target="tpu_custom_call" | custom-call | tf_op jit(solution)/shard_map/pallas_call | solution.py:80
  222.4 2.0 convolution_multiply_fusion.1
  (140 shorter events, 51.7 us)
Async XLA Ops:
  7.4 1.6 copy-start
  7.4 7.0 %copy-start.24 = (bf16[16,1024]{1,0:T(8,128)(2,1)S(1)}, bf16[16,1024]{1,0:T(8,128)(2,1)}, u32[]{:S(2)}) copy-start(bf16[16,1024]{1,0:T(8,128)(2,1)} %param.11) | copy-start | bytes 98308
  7.4 41.4 %all-reduce.5.cloned.1.call-start = ((), (), s32[]{:S(2)}) async-start(), calls=%async_computation.1 | async-start | bytes 262144 | tf_op jit(solution)/shard_map/psum | solution.py:166
  13.7 79.0 %all-gather.3.cloned.1.call-start = ((), (), s32[]{:S(2)}) async-start(), calls=%async_computation.2 | async-start | bytes 4325376 | tf_op jit(solution)/shard_map/all_gather | solution.py:153
  14.3 208.1 %all-reduce.3.cloned.1.call-start = ((), (), s32[]{:S(2)}) async-start(), calls=%async_computation | async-start | bytes 1048576 | tf_op jit(solution)/shard_map/psum | solution.py:146
  92.7 25.5 %copy-start.11 = (f32[32,1024]{1,0:T(8,128)}, f32[32,1024]{1,0:T(8,128)S(1)}, u32[]{:S(2)}) copy-start(f32[32,1024]{1,0:T(8,128)S(1)} %reshape_squeeze.3) | copy-start | bytes 393220
  101.4 2.9 %copy-start.6 = (f32[4096,256]{1,0:T(8,128)S(1)}, f32[4096,256]{1,0:T(8,128)}, u32[]{:S(2)}) copy-start(f32[4096,256]{1,0:T(8,128)} %all-gather.3.cloned.1.call-done) | copy-start | bytes 12582916
  102.6 15.6 %copy-start.17 = (f32[32,128]{1,0:T(8,128)}, f32[32,128]{1,0:T(8,128)S(1)}, u32[]{:S(2)}) copy-start(f32[32,128]{1,0:T(8,128)S(1)} %fusion.49) | copy-start | bytes 49156
  108.7 1.7 copy-start.1
  121.4 5.8 %copy-start.19 = (f32[128,32]{0,1:T(8,128)}, f32[128,32]{0,1:T(8,128)S(1)}, u32[]{:S(2)}) copy-start(f32[128,32]{0,1:T(8,128)S(1)} %fusion.47) | copy-start | bytes 49156
  125.1 1.4 copy-start.2
  148.8 4.7 %copy-start.16 = (f32[640,32]{0,1:T(8,128)S(1)}, f32[640,32]{0,1:T(8,128)}, u32[]{:S(2)}) copy-start(f32[640,32]{0,1:T(8,128)} %convolution_subtract_fusion.5) | copy-start | bytes 245764
  151.2 3.3 %copy-start.20 = (f32[128,32]{0,1:T(8,128)}, f32[128,32]{0,1:T(8,128)S(1)}, u32[]{:S(2)}) copy-start(f32[128,32]{0,1:T(8,128)S(1)} %fusion.43) | copy-start | bytes 49156
  163.6 2.9 %copy-start.4 = (f32[384,128]{1,0:T(8,128)}, f32[384,128]{1,0:T(8,128)S(1)}, u32[]{:S(2)}) copy-start(f32[384,128]{1,0:T(8,128)S(1)} %fusion.11) | copy-start | bytes 589828
  164.7 3.6 %copy-start.21 = (f32[128,32]{0,1:T(8,128)}, f32[128,32]{0,1:T(8,128)S(1)}, u32[]{:S(2)}) copy-start(f32[128,32]{0,1:T(8,128)S(1)} %fusion.41) | copy-start | bytes 49156
  166.5 1.8 copy-start.9
  177.4 2.5 %copy-start.7 = (f32[256,128]{1,0:T(8,128)}, f32[256,128]{1,0:T(8,128)S(1)}, u32[]{:S(2)}) copy-start(f32[256,128]{1,0:T(8,128)S(1)} %fusion.13) | copy-start | bytes 393220
  178.5 3.0 %copy-start.23 = (f32[128,32]{0,1:T(8,128)}, f32[128,32]{0,1:T(8,128)S(1)}, u32[]{:S(2)}) copy-start(f32[128,32]{0,1:T(8,128)S(1)} %fusion.39) | copy-start | bytes 49156
  179.8 1.6 copy-start.15
  190.5 2.8 %copy-start.10 = (f32[128,128]{1,0:T(8,128)}, f32[128,128]{1,0:T(8,128)S(1)}, u32[]{:S(2)}) copy-start(f32[128,128]{1,0:T(8,128)S(1)} %fusion.17) | copy-start | bytes 196612
  191.5 1.8 copy-start.22
  202.1 14.1 %copy-start.18 = (f32[32,128]{1,0:T(8,128)S(1)}, f32[32,128]{1,0:T(8,128)}, u32[]{:S(2)}) copy-start(f32[32,128]{1,0:T(8,128)} %copy-done.17) | copy-start | bytes 49156
  202.1 14.5 %copy-start.14 = (f32[128,128]{1,0:T(8,128)S(1)}, f32[128,128]{1,0:T(8,128)}, u32[]{:S(2)}) copy-start(f32[128,128]{1,0:T(8,128)} %shard_map.64) | copy-start | bytes 196612
  202.1 14.8 %copy-start.12 = (f32[32,1024]{1,0:T(8,128)S(1)}, f32[32,1024]{1,0:T(8,128)}, u32[]{:S(2)}) copy-start(f32[32,1024]{1,0:T(8,128)} %copy-done.11) | copy-start | bytes 393220
  (4 other events, 3.9 us)
Sparse Core Ops, SparseCore 0:
  13.8 34.9 all-reduce.4
  52.6 79.8 all-reduce.2
Sparse Core Ops, SparseCore 1:
  17.0 66.4 all-gather.2

commit v6 on v4

--- a/solution.py
+++ b/solution.py
@@ -163,11 +163,24 @@
     factor_in = jnp.einsum("eld,dk->ekl", activations, proj_in, preferred_element_type=jnp.float32)
     factor_out = jnp.einsum("eld,dk->ekl", out_grads, proj_out, preferred_element_type=jnp.float32)
     factors = jnp.concatenate((factor_in, factor_out), axis=1)
-    factors = lax.psum(factors, "param")
-    summed = outer_terms(factors, in_width)
-    features = (summed * (1.0 / math.sqrt(tokens))).astype(jnp.bfloat16)
-    local_count, feat_dim = features.shape
-    all_features = gather_rows(features.astype(jnp.float32), "ex")
+    local_count = factors.shape[0]
+    n_ex = lax.axis_size("ex")
+    if n_ex * factors.size * 4 <= (2 << 20):
+        padded = jnp.zeros((n_ex * local_count,) + factors.shape[1:], factors.dtype)
+        padded = lax.dynamic_update_slice_in_dim(padded, factors, lax.axis_index("ex") * local_count, 0)
+        all_factors = lax.psum(padded, ("ex", "param"))
+        summed = outer_terms(all_factors, in_width)
+        features = (summed * (1.0 / math.sqrt(tokens))).astype(jnp.bfloat16)
+        feat_dim = features.shape[1]
+        all_features = features.astype(jnp.float32)
+    else:
+        factors = lax.psum(factors, "param")
+        summed = outer_terms(factors, in_width)
+        features = (summed * (1.0 / math.sqrt(tokens))).astype(jnp.bfloat16)
+        feat_dim = features.shape[1]
+        everyone = lax.all_gather(features.astype(jnp.float32), ("ex", "param"), axis=0, tiled=False)
+        all_features = everyone.reshape(n_ex, lax.axis_size("param"), local_count, feat_dim)[:, 0]
+        all_features = all_features.reshape(-1, feat_dim)
     train_count = all_features.shape[0]
     block = 128 if feat_dim % 128 == 0 else feat_dim
     inverses, panels = blocked_cholesky(full_prior, block)

time: 265 us -> 351 us (1.32)
  waiting for transfers between devices: 108 us -> 194 us
    psum x1, waiting for transfers between devices: 34.4 us -> 131 us  [per_device(): all_factors = lax.psum(padded, ('ex', 'param'))]
    psum x1, waiting for transfers between devices: 41.3 us -> 0.02 us  [gather_rows(): return lax.psum(padded, axis_name)]
    all_gather x1, waiting for transfers between devices: 32.2 us -> 61.9 us  [gather_prior(): blocks = lax.all_gather(prior, ('ex', 'param'), axis=0, tiled=False)]
  transfers between devices with their start and end apart: 3 -> 3, of which waited for: 3 -> 2; matrix products, arithmetic and copies ran while one was open for 1% -> 19% of each run, Pallas kernels for 3% -> 17%
where the time goes in v6:
time: 351 us; the launch traced here: 349 us
  waiting for transfers between devices  194 us (55%)
  matrix products  65.9 us (19%)
  Pallas kernels  60.6 us (17%)
  local copies, waits for them, and re-layouts  14.2 us (4%)
  between operations  13.9 us (4%)
    psum x1, waiting for transfers between devices, per_device(): all_factors = lax.psum(padded, ('ex', 'param'))  131 us
    all_gather x1, waiting for transfers between devices, gather_prior(): blocks = lax.all_gather(prior, ('ex', 'param'), axis=0, tiled=False)  61.9 us
    pallas_call x9, Pallas kernels, inverse_factor(): pl.pallas_call(functools.partial(_inverse_factor_kernel, width), out_shap...  60.6 us
    dot_general x47, matrix products, mm(): jnp.dot(a, b, precision=lax.Precision.HIGHEST, preferred_element_type=jnp...  58.9 us
  transfers between devices with their start and end apart: 3, of which 2 were waited for; matrix products, arithmetic and copies ran while one was open for 19% of the time, Pallas kernels for 17%

profile of v6, /device:TPU:0, one launch (start us, length us, event | category | flops | bytes accessed | tf_op | source)
XLA Modules:
  0.0 348.7 jit_solution(13852508490104583752)
XLA Ops:
  8.1 1.6 convolution_bitcast_fusion.1
  9.8 2.4 convolution_bitcast_fusion
  15.0 131.0 %all-reduce.5.cloned.1.call-done = f32[32,64,128]{2,1,0:T(8,128)} async-done(((f32[32,64,128]{2,1,0:T(8,128)}), f32[32,64,128]{2,1,0:T(8,128)}) %all-reduce.5.cloned.1.call-update) | async-done | bytes 1048592 | tf_op jit(solution)/shard_map/psum | solution.py:171
  146.0 2.1 fusion
  148.5 61.9 %all-gather.3.cloned.1.call-done = f32[4096,256]{1,0:T(8,128)} async-done(((f32[128,256]{1,0:T(8,128)}), f32[4096,256]{1,0:T(8,128)}) %all-gather.3.cloned.1.call-update) | async-done | bytes 4194320 | tf_op jit(solution)/shard_map/all_gather | solution.py:153
  211.8 7.4 %shard_map.64 = f32[128,128]{1,0:T(8,128)} custom-call(f32[128,128]{1,0:T(8,128)} %slice.306.a_ref), custom_call_target="tpu_custom_call" | custom-call | tf_op jit(solution)/shard_map/pallas_call | solution.py:80
  223.6 2.8 slice_subtract_fusion
  226.5 1.6 copy-done.1
  228.7 7.2 %shard_map.65 = f32[128,128]{1,0:T(8,128)} custom-call(f32[128,128]{1,0:T(8,128)} %slice.337.a_ref), custom_call_target="tpu_custom_call" | custom-call | tf_op jit(solution)/shard_map/pallas_call | solution.py:80
  239.1 3.7 %slice_subtract_fusion.1 = f32[768,768]{1,0:T(8,128)S(1)} fusion(f32[896,896]{1,0:T(8,128)} %copy-done.1, f32[768,128]{1,0:T(8,128)S(1)} %fusion.6), kind=kOutput, calls=%fused_computation.1 | convolution fusion | flops 906559488 | bytes 5505024 | tf_op jit(solution)/shard_map/dot_general | solution.py:105
  244.9 7.2 %shard_map.66 = f32[128,128]{1,0:T(8,128)} custom-call(f32[128,128]{1,0:T(8,128)} %slice.342.a_ref), custom_call_target="tpu_custom_call" | custom-call | tf_op jit(solution)/shard_map/pallas_call | solution.py:80
  254.6 2.9 slice_subtract_fusion.2
  259.3 7.2 %shard_map.67 = f32[128,128]{1,0:T(8,128)} custom-call(f32[128,128]{1,0:T(8,128)} %slice.347.a_ref), custom_call_target="tpu_custom_call" | custom-call | tf_op jit(solution)/shard_map/pallas_call | solution.py:80
  269.0 2.3 convolution_subtract_fusion
  272.9 7.2 %shard_map.68 = f32[128,128]{1,0:T(8,128)} custom-call(f32[128,128]{1,0:T(8,128)} %slice.352.a_ref), custom_call_target="tpu_custom_call" | custom-call | tf_op jit(solution)/shard_map/pallas_call | solution.py:80
  282.6 1.7 convolution_subtract_fusion.1
  284.3 1.8 convolution_subtract_fusion.8
  286.8 7.2 %shard_map.69 = f32[128,128]{1,0:T(8,128)} custom-call(f32[128,128]{1,0:T(8,128)} %slice.357.a_ref), custom_call_target="tpu_custom_call" | custom-call | tf_op jit(solution)/shard_map/pallas_call | solution.py:80
  297.6 1.6 convolution_subtract_fusion.9
  299.9 7.2 %shard_map.70 = f32[128,128]{1,0:T(8,128)} custom-call(f32[128,128]{1,0:T(8,128)} %slice.362.a_ref), custom_call_target="tpu_custom_call" | custom-call | tf_op jit(solution)/shard_map/pallas_call | solution.py:80
  309.4 1.7 convolution_subtract_fusion.6.a_ref
  312.7 7.2 %shard_map.71 = f32[128,128]{1,0:T(8,128)} custom-call(f32[128,128]{1,0:T(8,128)} %convolution_subtract_fusion.6.a_ref), custom_call_target="tpu_custom_call" | custom-call | tf_op jit(solution)/shard_map/pallas_call | solution.py:80
  335.5 2.6 shard_map.72
  340.1 2.0 convolution_multiply_fusion.1
  (140 shorter events, 52.9 us)
Async XLA Ops:
  6.5 1.6 copy-start
  6.5 139.5 %all-reduce.5.cloned.1.call-start = ((), (), s32[]{:S(2)}) async-start(), calls=%async_computation.1 | async-start | bytes 2097152 | tf_op jit(solution)/shard_map/psum | solution.py:171
  9.8 4.5 %copy-start.25 = (bf16[16,1024]{1,0:T(8,128)(2,1)S(1)}, bf16[16,1024]{1,0:T(8,128)(2,1)}, u32[]{:S(2)}) copy-start(bf16[16,1024]{1,0:T(8,128)(2,1)} %param.11) | copy-start | bytes 98308
  13.4 197.0 %all-gather.3.cloned.1.call-start = ((), (), s32[]{:S(2)}) async-start(), calls=%async_computation.2 | async-start | bytes 4325376 | tf_op jit(solution)/shard_map/all_gather | solution.py:153
  14.1 326.0 %all-reduce.3.cloned.1.call-start = ((), (), s32[]{:S(2)}) async-start(), calls=%async_computation | async-start | bytes 1048576 | tf_op jit(solution)/shard_map/psum | solution.py:146
  148.4 87.5 %copy-start.15 = (bf16[32,1024]{1,0:T(8,128)(2,1)}, bf16[32,1024]{1,0:T(8,128)(2,1)S(1)}, u32[]{:S(2)}) copy-start(bf16[32,1024]{1,0:T(8,128)(2,1)S(1)} %convert_element_type.17) | copy-start | bytes 196612
  219.2 2.8 copy-start.7
  220.3 15.6 %copy-start.18 = (f32[32,128]{1,0:T(8,128)}, f32[32,128]{1,0:T(8,128)S(1)}, u32[]{:S(2)}) copy-start(f32[32,128]{1,0:T(8,128)S(1)} %fusion.50) | copy-start | bytes 49156
  226.5 1.7 copy-start.1
  239.1 5.8 %copy-start.20 = (f32[128,32]{0,1:T(8,128)}, f32[128,32]{0,1:T(8,128)S(1)}, u32[]{:S(2)}) copy-start(f32[128,32]{0,1:T(8,128)S(1)} %fusion.46) | copy-start | bytes 49156
  242.8 1.4 copy-start.2
  266.5 4.7 %copy-start.17 = (f32[640,32]{0,1:T(8,128)S(1)}, f32[640,32]{0,1:T(8,128)}, u32[]{:S(2)}) copy-start(f32[640,32]{0,1:T(8,128)} %convolution_subtract_fusion.5) | copy-start | bytes 245764
  269.0 3.3 copy-start.21
  281.4 2.9 copy-start.4
  282.5 3.6 %copy-start.22 = (f32[128,32]{0,1:T(8,128)}, f32[128,32]{0,1:T(8,128)S(1)}, u32[]{:S(2)}) copy-start(f32[128,32]{0,1:T(8,128)S(1)} %fusion.40) | copy-start | bytes 49156
  284.3 1.8 copy-start.10
  295.2 2.5 copy-start.8
  296.3 3.0 copy-start.24
  297.6 1.6 copy-start.14
  308.3 2.9 copy-start.11
  309.4 1.8 copy-start.23
  319.9 14.1 %copy-start.19 = (f32[32,128]{1,0:T(8,128)S(1)}, f32[32,128]{1,0:T(8,128)}, u32[]{:S(2)}) copy-start(f32[32,128]{1,0:T(8,128)} %copy-done.18) | copy-start | bytes 49156
  319.9 14.5 %copy-start.13 = (f32[128,128]{1,0:T(8,128)S(1)}, f32[128,128]{1,0:T(8,128)}, u32[]{:S(2)}) copy-start(f32[128,128]{1,0:T(8,128)} %shard_map.64) | copy-start | bytes 196612
  319.9 14.8 %copy-start.16 = (bf16[32,1024]{1,0:T(8,128)(2,1)S(1)}, bf16[32,1024]{1,0:T(8,128)(2,1)}, u32[]{:S(2)}) copy-start(bf16[32,1024]{1,0:T(8,128)(2,1)} %copy-done.15) | copy-start | bytes 196612
  (5 other events, 4.9 us)
Sparse Core Ops, SparseCore 0:
  13.5 132.5 all-reduce.4
  149.3 60.9 all-gather.2
  214.1 70.8 all-reduce.2

commit v7 on v4

--- a/solution.py
+++ b/solution.py
@@ -171,7 +171,8 @@
     train_count = all_features.shape[0]
     block = 128 if feat_dim % 128 == 0 else feat_dim
     inverses, panels = blocked_cholesky(full_prior, block)
-    prior_solved_t = blocked_solve(inverses, panels, all_features.T, block)
+    later = inverses[len(inverses) // 2][:1, :1]
+    prior_solved_t = blocked_solve(inverses, panels, all_features.T + 0.0 * later, block)
     gram = jnp.dot(all_features, prior_solved_t, precision=lax.Precision.HIGHEST)
     small = gram + train_count * jnp.eye(train_count, dtype=jnp.float32)
     small_inverse = inverse_factor(small)

time: 265 us -> 227 us (0.86)
  waiting for transfers between devices: 108 us -> 67.2 us
  local copies, waits for them, and re-layouts: 12.7 us -> 17.9 us
  matrix products: 63.9 us -> 61.1 us
    psum x1, waiting for transfers between devices: 41.3 us -> 0.01 us  [gather_rows(): return lax.psum(padded, axis_name)]
    unnamed x72 -> x70, local copies, waits for them, and re-layouts: 5.62 us -> 9.5 us
    dot_general x47, matrix products: 57.9 us -> 55.1 us  [mm(): jnp.dot(a, b, precision=lax.Precision.HIGHEST, preferred_element_type=jnp...]
  transfers between devices with their start and end apart: 3 -> 3, of which waited for: 3 -> 2; matrix products, arithmetic and copies ran while one was open for 1% -> 12% of each run, Pallas kernels for 3% -> 16%
where the time goes in v7:
time: 227 us; the launch traced here: 225 us
  waiting for transfers between devices  67.2 us (30%)
  matrix products  61.1 us (27%)
  Pallas kernels  60.6 us (27%)
  local copies, waits for them, and re-layouts  17.9 us (8%)
  between operations  16.3 us (7%)
    pallas_call x9, Pallas kernels, inverse_factor(): pl.pallas_call(functools.partial(_inverse_factor_kernel, width), out_shap...  60.6 us
    dot_general x47, matrix products, mm(): jnp.dot(a, b, precision=lax.Precision.HIGHEST, preferred_element_type=jnp...  55.1 us
    psum x1, waiting for transfers between devices, per_device(): factors = lax.psum(factors, 'param')  34.4 us
    all_gather x1, waiting for transfers between devices, gather_prior(): blocks = lax.all_gather(prior, ('ex', 'param'), axis=0, tiled=False)  32.2 us
    unnamed x70, local copies, waits for them, and re-layouts  9.5 us
    slice x7, local copies, waits for them, and re-layouts, blocked_cholesky(): inverse = inverse_factor(trailing[:block, :block])  5.25 us
  transfers between devices with their start and end apart: 3, of which 2 were waited for; matrix products, arithmetic and copies ran while one was open for 12% of the time, Pallas kernels for 16%

profile of v7, /device:TPU:0, one launch (start us, length us, event | category | flops | bytes accessed | tf_op | source)
XLA Modules:
  0.0 225.2 jit_solution(2105817736056688381)
XLA Ops:
  7.4 1.6 copy-done
  9.0 1.6 convolution_bitcast_fusion.1
  10.6 2.4 %convolution_bitcast_fusion = f32[4,32,128]{2,1,0:T(8,128)S(1)} fusion(bf16[4,128,2048]{2,1,0:T(8,128)(2,1)} %param.7, bf16[2048,32]{0,1:T(8,128)(2,1)} %param.9), kind=kOutput, calls=%fused_computation.12 | convolution fusion | flops 67108864 | bytes 2293760 | tf_op jit(solution)/shard_map/eld,dk->ekl/dot_general | solution.py:164
  14.4 34.4 %all-reduce.4.cloned.1.call-done = f32[4,64,128]{2,1,0:T(8,128)} async-done(((f32[4,64,128]{2,1,0:T(8,128)}), f32[4,64,128]{2,1,0:T(8,128)}) %all-reduce.4.cloned.1.call-update) | async-done | bytes 131088 | tf_op jit(solution)/shard_map/psum | solution.py:166
  50.7 32.2 %all-gather.3.cloned.1.call-done = f32[4096,256]{1,0:T(8,128)} async-done(((f32[128,256]{1,0:T(8,128)}), f32[4096,256]{1,0:T(8,128)}) %all-gather.3.cloned.1.call-update) | async-done | bytes 4194320 | tf_op jit(solution)/shard_map/all_gather | solution.py:153
  84.4 7.2 %shard_map.64 = f32[128,128]{1,0:T(8,128)} custom-call(f32[128,128]{1,0:T(8,128)} %slice.335.a_ref), custom_call_target="tpu_custom_call" | custom-call | tf_op jit(solution)/shard_map/pallas_call | solution.py:80
  91.7 1.6 fusion.59
  95.8 2.8 %slice_subtract_fusion = f32[896,896]{1,0:T(8,128)S(1)} fusion(f32[896,1024]{1,0:T(8,128)S(1)} %maximum_dynamic-update-slice_fusion, f32[896,128]{1,0:T(8,128)S(1)} %fusion.3), kind=kOutput, calls=%fused_computation | convolution fusion | flops 1233928192 | bytes 7340032 | tf_op jit(solution)/shard_map/dot_general | solution.py:105
  98.7 1.6 copy-done.1
  101.0 7.2 %shard_map.65 = f32[128,128]{1,0:T(8,128)} custom-call(f32[128,128]{1,0:T(8,128)} %slice.338.a_ref), custom_call_target="tpu_custom_call" | custom-call | tf_op jit(solution)/shard_map/pallas_call | solution.py:80
  109.7 3.7 %slice_subtract_fusion.1 = f32[768,768]{1,0:T(8,128)S(1)} fusion(f32[896,896]{1,0:T(8,128)} %copy-done.1, f32[768,128]{1,0:T(8,128)S(1)} %fusion.5), kind=kOutput, calls=%fused_computation.1 | convolution fusion | flops 906559488 | bytes 5505024 | tf_op jit(solution)/shard_map/dot_general | solution.py:105
  115.4 7.2 %shard_map.66 = f32[128,128]{1,0:T(8,128)} custom-call(f32[128,128]{1,0:T(8,128)} %slice.341.a_ref), custom_call_target="tpu_custom_call" | custom-call | tf_op jit(solution)/shard_map/pallas_call | solution.py:80
  124.0 2.9 %slice_subtract_fusion.2 = f32[640,640]{1,0:T(8,128)S(1)} fusion(f32[768,768]{1,0:T(8,128)} %copy-done.2, f32[640,128]{1,0:T(8,128)S(1)} %fusion.7), kind=kOutput, calls=%fused_computation.2 | convolution fusion | flops 629555200 | bytes 3932160 | tf_op jit(solution)/shard_map/dot_general | solution.py:105
  128.8 7.2 %shard_map.67 = f32[128,128]{1,0:T(8,128)} custom-call(f32[128,128]{1,0:T(8,128)} %slice.344.a_ref), custom_call_target="tpu_custom_call" | custom-call | tf_op jit(solution)/shard_map/pallas_call | solution.py:80
  137.3 2.3 convolution_subtract_fusion
  141.2 7.4 %shard_map.68 = f32[128,128]{1,0:T(8,128)} custom-call(f32[128,128]{1,0:T(8,128)} %slice.345.a_ref), custom_call_target="tpu_custom_call" | custom-call | tf_op jit(solution)/shard_map/pallas_call | solution.py:80
  150.4 2.0 fusion.11
  163.2 7.2 %shard_map.69 = f32[128,128]{1,0:T(8,128)} custom-call(f32[128,128]{1,0:T(8,128)} %slice.358.a_ref), custom_call_target="tpu_custom_call" | custom-call | tf_op jit(solution)/shard_map/pallas_call | solution.py:80
  174.2 1.6 convolution_subtract_fusion.9
  176.4 7.2 %shard_map.70 = f32[128,128]{1,0:T(8,128)} custom-call(f32[128,128]{1,0:T(8,128)} %slice.363.a_ref), custom_call_target="tpu_custom_call" | custom-call | tf_op jit(solution)/shard_map/pallas_call | solution.py:80
  185.9 1.7 convolution_subtract_fusion.6.a_ref
  187.7 1.5 convolution_subtract_fusion.14
  189.2 7.2 %shard_map.71 = f32[128,128]{1,0:T(8,128)} custom-call(f32[128,128]{1,0:T(8,128)} %convolution_subtract_fusion.6.a_ref), custom_call_target="tpu_custom_call" | custom-call | tf_op jit(solution)/shard_map/pallas_call | solution.py:80
  212.2 2.6 %shard_map.72 = f32[32,32]{1,0:T(8,128)} custom-call(f32[32,32]{1,0:T(8,128)} %convolution_add_fusion.a_ref), custom_call_target="tpu_custom_call" | custom-call | tf_op jit(solution)/shard_map/pallas_call | solution.py:80
  (143 shorter events, 54.3 us)
Async XLA Ops:
  7.4 1.6 copy-start
  7.4 7.0 %copy-start.25 = (bf16[16,1024]{1,0:T(8,128)(2,1)S(1)}, bf16[16,1024]{1,0:T(8,128)(2,1)}, u32[]{:S(2)}) copy-start(bf16[16,1024]{1,0:T(8,128)(2,1)} %param.11) | copy-start | bytes 98308
  7.4 41.4 %all-reduce.4.cloned.1.call-start = ((), (), s32[]{:S(2)}) async-start(), calls=%async_computation | async-start | bytes 262144 | tf_op jit(solution)/shard_map/psum | solution.py:166
  13.7 69.2 %all-gather.3.cloned.1.call-start = ((), (), s32[]{:S(2)}) async-start(), calls=%async_computation.1 | async-start | bytes 4325376 | tf_op jit(solution)/shard_map/all_gather | solution.py:153
  14.3 138.1 %all-reduce.6.cloned.1.call-start = ((), (), s32[]{:S(2)}) async-start(), calls=%async_computation.2 | async-start | bytes 1310720 | tf_op jit(solution)/shard_map/psum | solution.py:146
  14.4 35.6 %copy-start.9 = (f32[128,1024]{1,0:T(8,128)}, f32[128,1024]{1,0:T(8,128)S(1)}, u32[]{:S(2)}) copy-start(f32[128,1024]{1,0:T(8,128)S(1)} %convert_dynamic-update-slice_fusion) | copy-start | bytes 1572868
  91.7 2.6 %copy-start.7 = (f32[4096,256]{1,0:T(8,128)S(1)}, f32[4096,256]{1,0:T(8,128)}, u32[]{:S(2)}) copy-start(f32[4096,256]{1,0:T(8,128)} %all-gather.3.cloned.1.call-done) | copy-start | bytes 12582916
  98.7 1.6 copy-start.1
  113.4 1.4 copy-start.2
  126.9 1.2 copy-start.3
  139.6 1.0 copy-start.5
  152.4 8.6 %copy-start.4 = (f32[384,128]{1,0:T(8,128)S(1)}, f32[384,128]{1,0:T(8,128)}, u32[]{:S(2)}) copy-start(f32[384,128]{1,0:T(8,128)} %fusion.11) | copy-start | bytes 589828
  152.4 8.6 %copy-start.6 = (f32[512,512]{1,0:T(8,128)S(1)}, f32[512,512]{1,0:T(8,128)}, u32[]{:S(2)}) copy-start(f32[512,512]{1,0:T(8,128)} %copy-done.5) | copy-start | bytes 3145732
  154.4 5.3 %copy-start.18 = (f32[32,128]{1,0:T(8,128)}, f32[32,128]{1,0:T(8,128)S(1)}, u32[]{:S(2)}) copy-start(f32[32,128]{1,0:T(8,128)S(1)} %fusion.49) | copy-start | bytes 49156
  161.0 1.6 copy-start.22
  171.7 2.5 %copy-start.8 = (f32[256,128]{1,0:T(8,128)}, f32[256,128]{1,0:T(8,128)S(1)}, u32[]{:S(2)}) copy-start(f32[256,128]{1,0:T(8,128)S(1)} %fusion.13) | copy-start | bytes 393220
  172.8 3.0 %copy-start.24 = (f32[128,32]{0,1:T(8,128)}, f32[128,32]{0,1:T(8,128)S(1)}, u32[]{:S(2)}) copy-start(f32[128,32]{0,1:T(8,128)S(1)} %fusion.39) | copy-start | bytes 49156
  174.1 1.7 copy-start.14
  184.8 2.9 %copy-start.11 = (f32[128,128]{1,0:T(8,128)}, f32[128,128]{1,0:T(8,128)S(1)}, u32[]{:S(2)}) copy-start(f32[128,128]{1,0:T(8,128)S(1)} %fusion.17) | copy-start | bytes 196612
  185.9 1.8 copy-start.23
  196.4 14.2 %copy-start.19 = (f32[32,128]{1,0:T(8,128)S(1)}, f32[32,128]{1,0:T(8,128)}, u32[]{:S(2)}) copy-start(f32[32,128]{1,0:T(8,128)} %copy-done.18) | copy-start | bytes 49156
  196.4 14.6 %copy-start.13 = (f32[128,128]{1,0:T(8,128)S(1)}, f32[128,128]{1,0:T(8,128)}, u32[]{:S(2)}) copy-start(f32[128,128]{1,0:T(8,128)} %shard_map.64) | copy-start | bytes 196612
  196.4 14.8 %copy-start.17 = (f32[32,1024]{1,0:T(8,128)S(1)}, f32[32,1024]{1,0:T(8,128)}, u32[]{:S(2)}) copy-start(f32[32,1024]{1,0:T(8,128)} %get-tuple-element.6) | copy-start | bytes 393220
  207.3 9.4 %copy-start.16 = (f32[128,1024]{1,0:T(8,128)S(1)}, f32[128,1024]{1,0:T(8,128)}, u32[]{:S(2)}) copy-start(f32[128,1024]{1,0:T(8,128)} %get-tuple-element.5) | copy-start | bytes 1572868
  (5 other events, 3.7 us)
Sparse Core Ops, SparseCore 0:
  13.8 34.9 all-reduce.3
  52.7 80.2 all-reduce.5
Sparse Core Ops, SparseCore 1:
  17.1 65.8 all-gather.2

commit v8 on v7

--- a/solution.py
+++ b/solution.py
@@ -20,7 +20,7 @@
     rows = lax.broadcasted_iota(jnp.int32, (n, n), 0)
     cols = lax.broadcasted_iota(jnp.int32, (n, n), 1)
     w_ref[...] = jnp.where(rows == cols, 1.0, 0.0).astype(jnp.float32)
-    segment = 32 if n % 32 == 0 else 8
+    segment = 16 if n % 16 == 0 else 8
     for group in range(n // segment):
         low = group * segment
 

time: 227 us -> 227 us (level)
  no operation moved by 1% of the time
where the time goes in v8:
time: 227 us; the launch traced here: 224 us
  waiting for transfers between devices  67.2 us (30%)
  matrix products  61.1 us (27%)
  Pallas kernels  59.7 us (26%)
  local copies, waits for them, and re-layouts  17.9 us (8%)
  between operations  16.3 us (7%)
    pallas_call x9, Pallas kernels, inverse_factor(): pl.pallas_call(functools.partial(_inverse_factor_kernel, width), out_shap...  59.7 us
    dot_general x47, matrix products, mm(): jnp.dot(a, b, precision=lax.Precision.HIGHEST, preferred_element_type=jnp...  55.1 us
    psum x1, waiting for transfers between devices, per_device(): factors = lax.psum(factors, 'param')  34.4 us
    all_gather x1, waiting for transfers between devices, gather_prior(): blocks = lax.all_gather(prior, ('ex', 'param'), axis=0, tiled=False)  32.2 us
    unnamed x70, local copies, waits for them, and re-layouts  9.5 us
    slice x7, local copies, waits for them, and re-layouts, blocked_cholesky(): inverse = inverse_factor(trailing[:block, :block])  5.25 us
  transfers between devices with their start and end apart: 3, of which 2 were waited for; matrix products, arithmetic and copies ran while one was open for 12% of the time, Pallas kernels for 16%

profile of v8, /device:TPU:0, one launch (start us, length us, event | category | flops | bytes accessed | tf_op | source)
XLA Modules:
  0.0 224.3 jit_solution(17016078014083618206)
XLA Ops:
  7.4 1.6 copy-done
  9.0 1.6 convolution_bitcast_fusion.1
  10.6 2.4 %convolution_bitcast_fusion = f32[4,32,128]{2,1,0:T(8,128)S(1)} fusion(bf16[4,128,2048]{2,1,0:T(8,128)(2,1)} %param.7, bf16[2048,32]{0,1:T(8,128)(2,1)} %param.9), kind=kOutput, calls=%fused_computation.12 | convolution fusion | flops 67108864 | bytes 2293760 | tf_op jit(solution)/shard_map/eld,dk->ekl/dot_general | solution.py:164
  14.4 34.4 %all-reduce.4.cloned.1.call-done = f32[4,64,128]{2,1,0:T(8,128)} async-done(((f32[4,64,128]{2,1,0:T(8,128)}), f32[4,64,128]{2,1,0:T(8,128)}) %all-reduce.4.cloned.1.call-update) | async-done | bytes 131088 | tf_op jit(solution)/shard_map/psum | solution.py:166
  50.7 32.2 %all-gather.3.cloned.1.call-done = f32[4096,256]{1,0:T(8,128)} async-done(((f32[128,256]{1,0:T(8,128)}), f32[4096,256]{1,0:T(8,128)}) %all-gather.3.cloned.1.call-update) | async-done | bytes 4194320 | tf_op jit(solution)/shard_map/all_gather | solution.py:153
  84.4 7.1 %shard_map.64 = f32[128,128]{1,0:T(8,128)} custom-call(f32[128,128]{1,0:T(8,128)} %slice.335.a_ref), custom_call_target="tpu_custom_call" | custom-call | tf_op jit(solution)/shard_map/pallas_call | solution.py:80
  91.6 1.6 fusion.59
  95.7 2.8 %slice_subtract_fusion = f32[896,896]{1,0:T(8,128)S(1)} fusion(f32[896,1024]{1,0:T(8,128)S(1)} %maximum_dynamic-update-slice_fusion, f32[896,128]{1,0:T(8,128)S(1)} %fusion.3), kind=kOutput, calls=%fused_computation | convolution fusion | flops 1233928192 | bytes 7340032 | tf_op jit(solution)/shard_map/dot_general | solution.py:105
  98.6 1.6 copy-done.1
  100.9 7.1 %shard_map.65 = f32[128,128]{1,0:T(8,128)} custom-call(f32[128,128]{1,0:T(8,128)} %slice.338.a_ref), custom_call_target="tpu_custom_call" | custom-call | tf_op jit(solution)/shard_map/pallas_call | solution.py:80
  109.4 3.7 %slice_subtract_fusion.1 = f32[768,768]{1,0:T(8,128)S(1)} fusion(f32[896,896]{1,0:T(8,128)} %copy-done.1, f32[768,128]{1,0:T(8,128)S(1)} %fusion.5), kind=kOutput, calls=%fused_computation.1 | convolution fusion | flops 906559488 | bytes 5505024 | tf_op jit(solution)/shard_map/dot_general | solution.py:105
  115.2 7.1 %shard_map.66 = f32[128,128]{1,0:T(8,128)} custom-call(f32[128,128]{1,0:T(8,128)} %slice.341.a_ref), custom_call_target="tpu_custom_call" | custom-call | tf_op jit(solution)/shard_map/pallas_call | solution.py:80
  123.7 2.9 %slice_subtract_fusion.2 = f32[640,640]{1,0:T(8,128)S(1)} fusion(f32[768,768]{1,0:T(8,128)} %copy-done.2, f32[640,128]{1,0:T(8,128)S(1)} %fusion.7), kind=kOutput, calls=%fused_computation.2 | convolution fusion | flops 629555200 | bytes 3932160 | tf_op jit(solution)/shard_map/dot_general | solution.py:105
  128.4 7.3 %shard_map.67 = f32[128,128]{1,0:T(8,128)} custom-call(f32[128,128]{1,0:T(8,128)} %slice.344.a_ref), custom_call_target="tpu_custom_call" | custom-call | tf_op jit(solution)/shard_map/pallas_call | solution.py:80
  137.1 2.2 %convolution_subtract_fusion = f32[512,512]{1,0:T(8,128)S(1)} fusion(f32[512,128]{1,0:T(8,128)S(1)} %fusion.9, f32[640,640]{1,0:T(8,128)} %copy-done.3), kind=kOutput, calls=%fused_computation.3 | convolution fusion | flops 402915328 | bytes 2621440 | tf_op jit(solution)/shard_map/dot_general | solution.py:105
  140.9 7.1 %shard_map.68 = f32[128,128]{1,0:T(8,128)} custom-call(f32[128,128]{1,0:T(8,128)} %slice.345.a_ref), custom_call_target="tpu_custom_call" | custom-call | tf_op jit(solution)/shard_map/pallas_call | solution.py:80
  149.9 2.0 fusion.11
  162.7 7.1 %shard_map.69 = f32[128,128]{1,0:T(8,128)} custom-call(f32[128,128]{1,0:T(8,128)} %slice.358.a_ref), custom_call_target="tpu_custom_call" | custom-call | tf_op jit(solution)/shard_map/pallas_call | solution.py:80
  173.5 1.6 convolution_subtract_fusion.9
  175.8 7.1 %shard_map.70 = f32[128,128]{1,0:T(8,128)} custom-call(f32[128,128]{1,0:T(8,128)} %slice.363.a_ref), custom_call_target="tpu_custom_call" | custom-call | tf_op jit(solution)/shard_map/pallas_call | solution.py:80
  185.1 1.7 convolution_subtract_fusion.6.a_ref
  186.9 1.5 convolution_subtract_fusion.14
  188.4 7.1 %shard_map.71 = f32[128,128]{1,0:T(8,128)} custom-call(f32[128,128]{1,0:T(8,128)} %convolution_subtract_fusion.6.a_ref), custom_call_target="tpu_custom_call" | custom-call | tf_op jit(solution)/shard_map/pallas_call | solution.py:80
  211.3 2.6 %shard_map.72 = f32[32,32]{1,0:T(8,128)} custom-call(f32[32,32]{1,0:T(8,128)} %convolution_add_fusion.a_ref), custom_call_target="tpu_custom_call" | custom-call | tf_op jit(solution)/shard_map/pallas_call | solution.py:80
  (143 shorter events, 54.2 us)
Async XLA Ops:
  7.4 1.6 copy-start
  7.4 7.0 %copy-start.25 = (bf16[16,1024]{1,0:T(8,128)(2,1)S(1)}, bf16[16,1024]{1,0:T(8,128)(2,1)}, u32[]{:S(2)}) copy-start(bf16[16,1024]{1,0:T(8,128)(2,1)} %param.11) | copy-start | bytes 98308
  7.4 41.4 %all-reduce.4.cloned.1.call-start = ((), (), s32[]{:S(2)}) async-start(), calls=%async_computation | async-start | bytes 262144 | tf_op jit(solution)/shard_map/psum | solution.py:166
  13.7 69.2 %all-gather.3.cloned.1.call-start = ((), (), s32[]{:S(2)}) async-start(), calls=%async_computation.1 | async-start | bytes 4325376 | tf_op jit(solution)/shard_map/all_gather | solution.py:153
  14.3 137.5 %all-reduce.6.cloned.1.call-start = ((), (), s32[]{:S(2)}) async-start(), calls=%async_computation.2 | async-start | bytes 1310720 | tf_op jit(solution)/shard_map/psum | solution.py:146
  14.4 35.6 %copy-start.9 = (f32[128,1024]{1,0:T(8,128)}, f32[128,1024]{1,0:T(8,128)S(1)}, u32[]{:S(2)}) copy-start(f32[128,1024]{1,0:T(8,128)S(1)} %convert_dynamic-update-slice_fusion) | copy-start | bytes 1572868
  91.5 2.6 %copy-start.7 = (f32[4096,256]{1,0:T(8,128)S(1)}, f32[4096,256]{1,0:T(8,128)}, u32[]{:S(2)}) copy-start(f32[4096,256]{1,0:T(8,128)} %all-gather.3.cloned.1.call-done) | copy-start | bytes 12582916
  98.6 1.6 copy-start.1
  113.1 1.4 copy-start.2
  126.6 1.2 copy-start.3
  139.3 1.0 copy-start.5
  151.8 8.6 %copy-start.4 = (f32[384,128]{1,0:T(8,128)S(1)}, f32[384,128]{1,0:T(8,128)}, u32[]{:S(2)}) copy-start(f32[384,128]{1,0:T(8,128)} %fusion.11) | copy-start | bytes 589828
  151.8 8.6 %copy-start.6 = (f32[512,512]{1,0:T(8,128)S(1)}, f32[512,512]{1,0:T(8,128)}, u32[]{:S(2)}) copy-start(f32[512,512]{1,0:T(8,128)} %copy-done.5) | copy-start | bytes 3145732
  153.9 5.3 %copy-start.18 = (f32[32,128]{1,0:T(8,128)}, f32[32,128]{1,0:T(8,128)S(1)}, u32[]{:S(2)}) copy-start(f32[32,128]{1,0:T(8,128)S(1)} %fusion.49) | copy-start | bytes 49156
  160.4 1.6 copy-start.22
  171.0 2.5 %copy-start.8 = (f32[256,128]{1,0:T(8,128)}, f32[256,128]{1,0:T(8,128)S(1)}, u32[]{:S(2)}) copy-start(f32[256,128]{1,0:T(8,128)S(1)} %fusion.13) | copy-start | bytes 393220
  172.1 3.0 %copy-start.24 = (f32[128,32]{0,1:T(8,128)}, f32[128,32]{0,1:T(8,128)S(1)}, u32[]{:S(2)}) copy-start(f32[128,32]{0,1:T(8,128)S(1)} %fusion.39) | copy-start | bytes 49156
  173.5 1.7 copy-start.14
  184.0 2.9 %copy-start.11 = (f32[128,128]{1,0:T(8,128)}, f32[128,128]{1,0:T(8,128)S(1)}, u32[]{:S(2)}) copy-start(f32[128,128]{1,0:T(8,128)S(1)} %fusion.17) | copy-start | bytes 196612
  185.1 1.8 copy-start.23
  195.6 14.2 %copy-start.19 = (f32[32,128]{1,0:T(8,128)S(1)}, f32[32,128]{1,0:T(8,128)}, u32[]{:S(2)}) copy-start(f32[32,128]{1,0:T(8,128)} %copy-done.18) | copy-start | bytes 49156
  195.6 14.6 %copy-start.13 = (f32[128,128]{1,0:T(8,128)S(1)}, f32[128,128]{1,0:T(8,128)}, u32[]{:S(2)}) copy-start(f32[128,128]{1,0:T(8,128)} %shard_map.64) | copy-start | bytes 196612
  195.6 14.8 %copy-start.17 = (f32[32,1024]{1,0:T(8,128)S(1)}, f32[32,1024]{1,0:T(8,128)}, u32[]{:S(2)}) copy-start(f32[32,1024]{1,0:T(8,128)} %get-tuple-element.6) | copy-start | bytes 393220
  206.5 9.4 %copy-start.16 = (f32[128,1024]{1,0:T(8,128)S(1)}, f32[128,1024]{1,0:T(8,128)}, u32[]{:S(2)}) copy-start(f32[128,1024]{1,0:T(8,128)} %get-tuple-element.5) | copy-start | bytes 1572868
  (5 other events, 3.7 us)
Sparse Core Ops, SparseCore 0:
  13.8 34.9 all-reduce.3
  52.7 80.2 all-reduce.5
Sparse Core Ops, SparseCore 1:
  17.1 65.8 all-gather.2

commit v9 on v8

--- a/solution.py
+++ b/solution.py
@@ -128,13 +128,12 @@
         parts.append(part)
         if k + 1 < count:
             rest = rest[block:] - mm(panels[k], part)
-    done = None
+    done = jnp.zeros((count * block,) + rhs.shape[1:], jnp.float32)
     for k in reversed(range(count)):
         target = parts[k]
-        if done is not None:
-            target = target - mm(panels[k].T, done)
-        part = mm(inverses[k].T, target)
-        done = part if done is None else jnp.concatenate((part, done), axis=0)
+        if k + 1 < count:
+            target = target - mm(panels[k].T, done[(k + 1) * block:])
+        done = lax.dynamic_update_slice_in_dim(done, mm(inverses[k].T, target), k * block, 0)
     return done
 
 

time: 227 us -> 229 us (level)
    unnamed x70 -> x50, local copies, waits for them, and re-layouts: 9.5 us -> 10.1 us
where the time goes in v9:
time: 229 us; the launch traced here: 227 us
  waiting for transfers between devices  67.2 us (29%)
  matrix products  63 us (28%)
  Pallas kernels  59.7 us (26%)
  local copies, waits for them, and re-layouts  18.4 us (8%)
  between operations  16.1 us (7%)
    pallas_call x9, Pallas kernels, inverse_factor(): pl.pallas_call(functools.partial(_inverse_factor_kernel, width), out_shap...  59.7 us
    dot_general x47, matrix products, mm(): jnp.dot(a, b, precision=lax.Precision.HIGHEST, preferred_element_type=jnp...  57 us
    psum x1, waiting for transfers between devices, per_device(): factors = lax.psum(factors, 'param')  34.4 us
    all_gather x1, waiting for transfers between devices, gather_prior(): blocks = lax.all_gather(prior, ('ex', 'param'), axis=0, tiled=False)  32.2 us
    unnamed x50, local copies, waits for them, and re-layouts  10.1 us
    slice x7, local copies, waits for them, and re-layouts, blocked_cholesky(): inverse = inverse_factor(trailing[:block, :block])  5.24 us
  transfers between devices with their start and end apart: 3, of which 2 were waited for; matrix products, arithmetic and copies ran while one was open for 12% of the time, Pallas kernels for 16%

profile of v9, /device:TPU:0, one launch (start us, length us, event | category | flops | bytes accessed | tf_op | source)
XLA Modules:
  0.0 226.5 jit_solution(8769038353896536247)
XLA Ops:
  7.4 1.6 copy-done
  9.0 1.6 convolution_bitcast_fusion.1
  10.6 2.4 %convolution_bitcast_fusion = f32[4,32,128]{2,1,0:T(8,128)S(1)} fusion(bf16[4,128,2048]{2,1,0:T(8,128)(2,1)} %param.7, bf16[2048,32]{0,1:T(8,128)(2,1)} %param.9), kind=kOutput, calls=%fused_computation.12 | convolution fusion | flops 67108864 | bytes 2293760 | tf_op jit(solution)/shard_map/eld,dk->ekl/dot_general | solution.py:163
  14.4 34.4 %all-reduce.5.cloned.1.call-done = f32[4,64,128]{2,1,0:T(8,128)} async-done(((f32[4,64,128]{2,1,0:T(8,128)}), f32[4,64,128]{2,1,0:T(8,128)}) %all-reduce.5.cloned.1.call-update) | async-done | bytes 131088 | tf_op jit(solution)/shard_map/psum | solution.py:165
  50.7 32.2 %all-gather.3.cloned.1.call-done = f32[4096,256]{1,0:T(8,128)} async-done(((f32[128,256]{1,0:T(8,128)}), f32[4096,256]{1,0:T(8,128)}) %all-gather.3.cloned.1.call-update) | async-done | bytes 4194320 | tf_op jit(solution)/shard_map/all_gather | solution.py:152
  84.4 7.1 %shard_map.64 = f32[128,128]{1,0:T(8,128)} custom-call(f32[128,128]{1,0:T(8,128)} %slice.360.a_ref), custom_call_target="tpu_custom_call" | custom-call | tf_op jit(solution)/shard_map/pallas_call | solution.py:80
  91.5 1.6 fusion.47
  95.7 2.8 %slice_subtract_fusion = f32[896,896]{1,0:T(8,128)S(1)} fusion(f32[896,1024]{1,0:T(8,128)S(1)} %maximum_dynamic-update-slice_fusion, f32[896,128]{1,0:T(8,128)S(1)} %fusion.3), kind=kOutput, calls=%fused_computation | convolution fusion | flops 1233928192 | bytes 7340032 | tf_op jit(solution)/shard_map/dot_general | solution.py:105
  98.6 1.6 copy-done.1
  100.9 7.1 %shard_map.65 = f32[128,128]{1,0:T(8,128)} custom-call(f32[128,128]{1,0:T(8,128)} %slice.363.a_ref), custom_call_target="tpu_custom_call" | custom-call | tf_op jit(solution)/shard_map/pallas_call | solution.py:80
  109.4 3.7 %slice_subtract_fusion.1 = f32[768,768]{1,0:T(8,128)S(1)} fusion(f32[896,896]{1,0:T(8,128)} %copy-done.1, f32[768,128]{1,0:T(8,128)S(1)} %fusion.5), kind=kOutput, calls=%fused_computation.1 | convolution fusion | flops 906559488 | bytes 5505024 | tf_op jit(solution)/shard_map/dot_general | solution.py:105
  115.2 7.1 %shard_map.66 = f32[128,128]{1,0:T(8,128)} custom-call(f32[128,128]{1,0:T(8,128)} %slice.366.a_ref), custom_call_target="tpu_custom_call" | custom-call | tf_op jit(solution)/shard_map/pallas_call | solution.py:80
  123.7 2.9 %slice_subtract_fusion.2 = f32[640,640]{1,0:T(8,128)S(1)} fusion(f32[768,768]{1,0:T(8,128)} %copy-done.2, f32[640,128]{1,0:T(8,128)S(1)} %fusion.7), kind=kOutput, calls=%fused_computation.2 | convolution fusion | flops 629555200 | bytes 3932160 | tf_op jit(solution)/shard_map/dot_general | solution.py:105
  128.4 7.3 %shard_map.67 = f32[128,128]{1,0:T(8,128)} custom-call(f32[128,128]{1,0:T(8,128)} %slice.369.a_ref), custom_call_target="tpu_custom_call" | custom-call | tf_op jit(solution)/shard_map/pallas_call | solution.py:80
  137.0 2.2 convolution_subtract_fusion
  140.9 7.1 %shard_map.68 = f32[128,128]{1,0:T(8,128)} custom-call(f32[128,128]{1,0:T(8,128)} %slice.372.a_ref), custom_call_target="tpu_custom_call" | custom-call | tf_op jit(solution)/shard_map/pallas_call | solution.py:80
  149.8 2.0 fusion.11
  162.7 7.1 %shard_map.69 = f32[128,128]{1,0:T(8,128)} custom-call(f32[128,128]{1,0:T(8,128)} %slice.375.a_ref), custom_call_target="tpu_custom_call" | custom-call | tf_op jit(solution)/shard_map/pallas_call | solution.py:80
  173.5 1.6 convolution_subtract_fusion.9
  175.7 7.1 %shard_map.70 = f32[128,128]{1,0:T(8,128)} custom-call(f32[128,128]{1,0:T(8,128)} %slice.378.a_ref), custom_call_target="tpu_custom_call" | custom-call | tf_op jit(solution)/shard_map/pallas_call | solution.py:80
  185.1 1.7 convolution_subtract_fusion.7.a_ref
  188.4 7.1 %shard_map.71 = f32[128,128]{1,0:T(8,128)} custom-call(f32[128,128]{1,0:T(8,128)} %convolution_subtract_fusion.7.a_ref), custom_call_target="tpu_custom_call" | custom-call | tf_op jit(solution)/shard_map/pallas_call | solution.py:80
  212.3 2.6 %shard_map.72 = f32[32,32]{1,0:T(8,128)} custom-call(f32[32,32]{1,0:T(8,128)} %convolution_add_fusion.a_ref), custom_call_target="tpu_custom_call" | custom-call | tf_op jit(solution)/shard_map/pallas_call | solution.py:80
  217.1 2.0 convolution_multiply_fusion.1
  (120 shorter events, 56.3 us)
Async XLA Ops:
  7.4 1.6 copy-start
  7.4 7.0 %copy-start.24 = (bf16[16,1024]{1,0:T(8,128)(2,1)S(1)}, bf16[16,1024]{1,0:T(8,128)(2,1)}, u32[]{:S(2)}) copy-start(bf16[16,1024]{1,0:T(8,128)(2,1)} %param.11) | copy-start | bytes 98308
  7.4 41.4 %all-reduce.5.cloned.1.call-start = ((), (), s32[]{:S(2)}) async-start(), calls=%async_computation | async-start | bytes 262144 | tf_op jit(solution)/shard_map/psum | solution.py:165
  13.7 69.2 %all-gather.3.cloned.1.call-start = ((), (), s32[]{:S(2)}) async-start(), calls=%async_computation.1 | async-start | bytes 4325376 | tf_op jit(solution)/shard_map/all_gather | solution.py:152
  14.3 137.5 %all-reduce.7.cloned.1.call-start = ((), (), s32[]{:S(2)}) async-start(), calls=%async_computation.2 | async-start | bytes 1310720 | tf_op jit(solution)/shard_map/psum | solution.py:145
  14.4 35.6 %copy-start.10 = (f32[128,1024]{1,0:T(8,128)}, f32[128,1024]{1,0:T(8,128)S(1)}, u32[]{:S(2)}) copy-start(f32[128,1024]{1,0:T(8,128)S(1)} %convert_dynamic-update-slice_fusion) | copy-start | bytes 1572868
  91.5 2.6 %copy-start.8 = (f32[4096,256]{1,0:T(8,128)S(1)}, f32[4096,256]{1,0:T(8,128)}, u32[]{:S(2)}) copy-start(f32[4096,256]{1,0:T(8,128)} %all-gather.3.cloned.1.call-done) | copy-start | bytes 12582916
  94.3 0.8 copy-start.13
  98.6 1.7 copy-start.1
  113.1 1.4 copy-start.2
  126.6 1.2 copy-start.3
  139.3 1.0 copy-start.6
  151.8 8.6 %copy-start.5 = (f32[384,128]{1,0:T(8,128)S(1)}, f32[384,128]{1,0:T(8,128)}, u32[]{:S(2)}) copy-start(f32[384,128]{1,0:T(8,128)} %fusion.11) | copy-start | bytes 589828
  151.8 8.6 %copy-start.7 = (f32[512,512]{1,0:T(8,128)S(1)}, f32[512,512]{1,0:T(8,128)}, u32[]{:S(2)}) copy-start(f32[512,512]{1,0:T(8,128)} %copy-done.6) | copy-start | bytes 3145732
  153.9 5.3 %copy-start.18 = (f32[32,128]{1,0:T(8,128)}, f32[32,128]{1,0:T(8,128)S(1)}, u32[]{:S(2)}) copy-start(f32[32,128]{1,0:T(8,128)S(1)} %fusion.40) | copy-start | bytes 49156
  160.4 1.6 copy-start.21
  161.1 1.0 copy-start.11
  171.0 2.5 %copy-start.9 = (f32[256,128]{1,0:T(8,128)}, f32[256,128]{1,0:T(8,128)S(1)}, u32[]{:S(2)}) copy-start(f32[256,128]{1,0:T(8,128)S(1)} %fusion.13) | copy-start | bytes 393220
  172.1 3.0 %copy-start.23 = (f32[128,32]{0,1:T(8,128)}, f32[128,32]{0,1:T(8,128)S(1)}, u32[]{:S(2)}) copy-start(f32[128,32]{0,1:T(8,128)S(1)} %fusion.30) | copy-start | bytes 49156
  173.5 1.7 copy-start.15
  184.0 2.8 %copy-start.12 = (f32[128,128]{1,0:T(8,128)}, f32[128,128]{1,0:T(8,128)S(1)}, u32[]{:S(2)}) copy-start(f32[128,128]{1,0:T(8,128)S(1)} %fusion.21) | copy-start | bytes 196612
  185.1 1.8 copy-start.22
  195.5 15.1 %copy-start.14 = (f32[128,128]{1,0:T(8,128)S(1)}, f32[128,128]{1,0:T(8,128)}, u32[]{:S(2)}) copy-start(f32[128,128]{1,0:T(8,128)} %shard_map.64) | copy-start | bytes 196612
  195.5 15.9 %copy-start.17 = (f32[32,1024]{1,0:T(8,128)S(1)}, f32[32,1024]{1,0:T(8,128)}, u32[]{:S(2)}) copy-start(f32[32,1024]{1,0:T(8,128)} %get-tuple-element.6) | copy-start | bytes 393220
  (4 other events, 2.6 us)
Sparse Core Ops, SparseCore 0:
  13.8 34.9 all-reduce.4
  52.7 80.2 all-reduce.6
Sparse Core Ops, SparseCore 1:
  17.1 65.8 all-gather.2
